TPU v7x, 512 devices: a whole 4x8x8 slice. The times are simulated.
512 devices in a mesh: grp: 8 (over z_hi, core), req: 64 (over y, x, z_lo).
Axes of the slice: x: 4, y: 8, z: 8 (z_hi: 4, z_lo: 2; z = z_hi * 2 + z_lo), core: 2. Of those that a mesh axis runs over, the one named last changes fastest.
Arguments:
- queries: bfloat16 [8, 64, 4, 2048], P('grp', 'req'), may hold values from -12 to 1700
- suffix_kv: bfloat16 [8, 64, 2, 4, 512], P('grp', 'req'), may hold values from -6 to 6
- prefix_pool: bfloat16 [8, 64, 3, 2, 128, 512], P('grp', 'req'), may hold values from -6 to 6
- page_table: int32 [64, 16], P('req'), may hold values from 0 to 23, as said below
- suffix_len: int32 [8, 64], P('grp'), may hold values from 1 to 4, 128 in all within a row
- residual: bfloat16 [8, 256, 4096], P('grp', None, 'req'), may hold values from -40 to 40
- out_weight: bfloat16 [2048, 4096], P(None, 'req'), may hold values from -0.5 to 0.5
- norm_gain: bfloat16 [4096], P('req'), may hold values from 0.099609375 to 1.8984375
- gate_up: bfloat16 [2, 4096, 8192], P(None, None, 'req'), may hold values from -0.09375 to 0.09375
- down_weight: bfloat16 [8192, 4096], P('req'), may hold values from -0.1875 to 0.1875
Outputs:
- hidden_out: bfloat16 [8, 256, 4096], P('grp', None, 'req')
Inputs may be any that keep to these rules, and one draw needn't show every extreme that they name: `page_table`: row b lists 16 different pages of group b's pool; pool page p is slot p % 3 on the member p // 3.
All inputs are finite; a program needn't handle non-finite values.
Results may differ from a plain program's by a relative error of at most 0.028.
Values may be sent and summed in bfloat16 or wider, within the bound.
No kernel may reach another device: no remote copies, remote signals or barrier semaphores. Data moves between devices by JAX's collectives and lax.ppermute only.
A program may use at most 64 MiB of HBM per device.

v0:
```python
import jax
import jax.numpy as jnp
from jax import lax
from jax.sharding import PartitionSpec as P

D = 4096
HD = 128
QH = 16
KVH = 4
PAGE = 128


def split_heads(query_rows):
    row_count = query_rows.shape[0]
    query_heads = query_rows.reshape(row_count, KVH, QH // KVH, HD)
    return jnp.transpose(query_heads, (1, 2, 0, 3))


def empty_state(row_count):
    running_max = jnp.full((KVH, QH // KVH, row_count), -1e30, jnp.float32)
    weight_sum = jnp.zeros((KVH, QH // KVH, row_count), jnp.float32)
    accumulated = jnp.zeros((KVH, QH // KVH, row_count, HD), jnp.float32)
    return (running_max, weight_sum, accumulated)


def page_block(softmax_state, pages_part, query_heads, table_row):
    running_max, weight_sum, accumulated = softmax_state
    page_count = pages_part.shape[0]
    page_index = jnp.arange(page_count, dtype=jnp.int32)
    page_used = jnp.any(page_index[:, None] == table_row[None, :], axis=1)
    token_live = jnp.repeat(page_used, PAGE)
    key_rows = pages_part[:, 0].reshape(page_count * PAGE, KVH, HD)
    value_rows = pages_part[:, 1].reshape(page_count * PAGE, KVH, HD)
    scores = jnp.einsum(
        "jgsd,tjd->jgst", query_heads, key_rows, preferred_element_type=jnp.float32
    ) * HD ** (-0.5)
    scores = jnp.where(token_live, scores, -1e30)
    merged_max = jnp.maximum(running_max, jnp.max(scores, axis=-1))
    weights = jnp.where(token_live, jnp.exp(scores - merged_max[..., None]), 0.0)
    weight_sum = jnp.sum(weights, axis=-1)
    weighted = jnp.einsum(
        "jgst,tjd->jgsd",
        weights.astype(jnp.bfloat16),
        value_rows,
        preferred_element_type=jnp.float32,
    )
    accumulated = weighted
    return (merged_max, weight_sum, accumulated)


def with_suffix(softmax_state, query_heads, own_suffix):
    running_max, weight_sum, accumulated = softmax_state
    row_count = query_heads.shape[2]
    key_rows = own_suffix[0].reshape(row_count, KVH, HD)
    value_rows = own_suffix[1].reshape(row_count, KVH, HD)
    scores = jnp.einsum(
        "jgsd,tjd->jgst", query_heads, key_rows, preferred_element_type=jnp.float32
    ) * HD ** (-0.5)
    causal = jnp.arange(row_count)[:, None] >= jnp.arange(row_count)[None, :]
    scores = jnp.where(causal, scores, -1e30)
    merged_max = jnp.maximum(running_max, jnp.max(scores, axis=-1))
    weights = jnp.where(causal, jnp.exp(scores - merged_max[..., None]), 0.0)
    rescale = jnp.exp(running_max - merged_max)
    weight_sum = weight_sum * rescale + jnp.sum(weights, axis=-1)
    weighted = jnp.einsum(
        "jgst,tjd->jgsd",
        weights.astype(jnp.bfloat16),
        value_rows,
        preferred_element_type=jnp.float32,
    )
    accumulated = accumulated * rescale[..., None] + weighted
    accumulated = accumulated / weight_sum[..., None]
    ordered = jnp.transpose(accumulated, (2, 0, 1, 3))
    return ordered.reshape(row_count, QH * HD).astype(jnp.bfloat16)


def body(
    queries,
    suffix_kv,
    prefix_pool,
    page_table,
    suffix_len,
    residual,
    out_weight,
    norm_gain,
    gate_up,
    down_weight,
):
    slot_count = queries.shape[2]
    own_queries = queries[0, 0]
    own_pool = prefix_pool[0, 0]
    table_row = page_table[0]
    own_heads = split_heads(own_queries)
    softmax_state = page_block(
        empty_state(slot_count),
        lax.all_gather(own_pool, "grp", axis=0, tiled=True),
        own_heads,
        table_row,
    )
    attention = with_suffix(softmax_state, own_heads, suffix_kv[0, 0])
    projected = jnp.dot(
        lax.all_gather(attention, "req", axis=0, tiled=True),
        out_weight,
        preferred_element_type=jnp.float32,
    )
    stream = (residual[0].astype(jnp.float32) + projected).astype(jnp.bfloat16)
    wide_local = stream.astype(jnp.float32)
    partial_sq = jnp.sum(wide_local * wide_local, axis=1)
    row_sumsq = lax.psum(partial_sq, "req")
    inverse_rms = lax.rsqrt(row_sumsq / D + 1e-05)
    normed = (wide_local * inverse_rms[:, None] * norm_gain.astype(jnp.float32)[None, :]).astype(
        jnp.bfloat16
    )
    gate_up_out = jnp.einsum(
        "nc,kcf->knf",
        lax.all_gather(normed, "req", axis=1, tiled=True),
        gate_up,
        preferred_element_type=jnp.float32,
    )
    hidden = (jax.nn.silu(gate_up_out[0]) * gate_up_out[1]).astype(jnp.bfloat16)
    partial_value = jnp.dot(hidden, down_weight, preferred_element_type=jnp.float32)
    summed = lax.psum_scatter(partial_value, "req", scatter_dimension=1, tiled=True)
    lengths = suffix_len[0]
    slot_index = jnp.arange(stream.shape[0], dtype=jnp.int32) % slot_count
    slot_live = (slot_index < jnp.repeat(lengths, slot_count)).astype(jnp.float32)
    result_rows = (wide_local + summed) * slot_live[:, None]
    return result_rows.astype(jnp.bfloat16)[None]


def solution(mesh):
    return jax.shard_map(
        body,
        mesh=mesh,
        in_specs=(
            P("grp", "req", None, None),
            P("grp", "req", None, None, None),
            P("grp", "req", None, None, None, None),
            P("req", None),
            P("grp", None),
            P("grp", None, "req"),
            P(None, "req"),
            P("req"),
            P(None, None, "req"),
            P("req", None),
        ),
        out_specs=P("grp", None, "req"),
        check_vma=False,
    )
```

profile of v0, /device:TPU:128, one launch (start us, length us, event | category | flops | bytes accessed | tf_op | source)
XLA Modules:
  0.0 1206.9 jit_solution(9325458423505003093)
XLA Ops:
  6.5 0.0 copy-start
  6.5 0.0 all-gather.8.cloned.1.call-start
  6.5 0.7 all-gather.8.cloned.1.call-update
  7.3 0.0 all-gather.10.cloned.1.call-start
  7.3 0.7 fusion.46
  8.1 0.1 broadcast_bitcast_fusion
  8.1 1.0 fusion.58
  9.1 76.7 %all-gather.8.cloned.1.call-done = bf16[1,1,24,2,128,512]{5,4,3,1,0,2:T(8,128)(2,1)} async-done(((bf16[1,1,3,2,128,512]{5,4,3,1,0,2:T(8,128)(2,1)}), bf16[1,1,24,2,128,512]{5,4,3,1,0,2:T(8,128)(2,1)}) %all-gather.8.cloned.1.call-update) | async-done | bytes 6291472 | tf_op jit(solution)/shard_map/all_gather | solution.py:96
  85.8 6.2 fusion.56
  92.0 0.0 copy-start.5
  92.0 5.5 reshape.67
  97.5 0.0 copy-start.6
  97.5 0.0 copy-done.5
  97.5 2.9 fusion.57
  100.5 0.0 copy-done.6
  100.5 0.2 convolution_bitcast_fusion
  100.7 5.5 reshape.68
  106.2 0.0 copy-start.7
  106.2 0.5 fusion.27
  106.7 0.0 copy-start.2
  106.8 0.0 copy-start.3
  106.8 3.4 fusion.24
  110.2 0.0 all-gather.10.cloned.1.call-update
  110.2 0.0 all-gather.6.cloned.1.call-start
  110.2 0.0 copy-done.7
  110.3 299.2 %all-gather.10.cloned.1.call-done = bf16[64,4,2048]{2,1,0:T(4,128)(2,1)} async-done(((bf16[1,4,2048]{2,1,0:T(4,128)(2,1)}), bf16[64,4,2048]{2,1,0:T(4,128)(2,1)}) %all-gather.10.cloned.1.call-update) | async-done | bytes 1048592 | tf_op jit(solution)/shard_map/all_gather | solution.py:102
  409.4 1.3 reshape.60
  410.8 0.0 copy-done.2
  410.8 0.0 copy-done.3
  410.8 0.5 multiply_reduce_fusion
  411.3 156.7 %psum.7 = f32[256]{0:T(256)S(1)} all-reduce(f32[256]{0:T(256)S(1)} %get-tuple-element.15), channel_id=1, replica_groups=mesh['grp'=8,'req'=64] {'req'}, use_global_device_ids=true, to_apply=%region_6.7 | all-reduce | flops 256 | bytes 2048 | tf_op jit(solution)/shard_map/psum | solution.py:109
  568.0 0.7 multiply_convert_fusion.1
  568.7 0.0 all-gather.6.cloned.1.call-update
  568.7 0.0 copy-start.1
  568.7 0.0 reduce-scatter.2.cloned.1.call-start
  568.7 298.6 %all-gather.6.cloned.1.call-done = bf16[256,4096]{0,1:T(8,128)(2,1)} async-done(((bf16[256,64]{0,1:T(8,128)(2,1)}), bf16[256,4096]{0,1:T(8,128)(2,1)}) %all-gather.6.cloned.1.call-update) | async-done | bytes 2097168 | tf_op jit(solution)/shard_map/all_gather | solution.py:116
  867.4 0.0 copy-done
  867.4 2.3 fusion.6
  869.7 0.0 copy-done.1
  869.7 2.7 fusion.35
  872.4 0.0 copy-start.4
  872.4 0.0 reduce-scatter.2.cloned.1.call-update
  872.4 0.6 copy-done.4
  873.1 0.1 broadcast_in_dim.56
  873.1 0.1 reshape.56
  873.3 325.7 %reduce-scatter.2.cloned.1.call-done = f32[256,64]{0,1:T(8,128)} async-done(((f32[256,4096]{0,1:T(8,128)}), f32[256,64]{0,1:T(8,128)}) %reduce-scatter.2.cloned.1.call-update) | async-done | bytes 65552 | tf_op jit(solution)/shard_map/reduce_scatter | solution.py:122
  1199.0 1.5 fusion.38
  (7 shorter events, 0.1 us)
Async XLA Ops:
  6.5 860.8 %copy-start = (bf16[2,4096,128]{2,1,0:T(8,128)(2,1)S(1)}, bf16[2,4096,128]{2,1,0:T(8,128)(2,1)}, u32[]{:S(2)}) copy-start(bf16[2,4096,128]{2,1,0:T(8,128)(2,1)} %param.18) | copy-start | bytes 6291460
  6.5 79.3 %all-gather.8.cloned.1.call-start = ((), (), s32[]{:S(2)}) async-start(), calls=%async_computation.3 | async-start | bytes 7077888 | tf_op jit(solution)/shard_map/all_gather | solution.py:96
  7.3 402.2 %all-gather.10.cloned.1.call-start = ((), (), s32[]{:S(2)}) async-start(), calls=%async_computation.4 | async-start | bytes 1064960 | tf_op jit(solution)/shard_map/all_gather | solution.py:102
  92.0 5.5 copy-start.5
  97.5 3.0 copy-start.6
  106.2 4.0 copy-start.7
  106.7 304.1 %copy-start.2 = (bf16[2048,64]{0,1:T(8,128)(2,1)S(1)}, bf16[2048,64]{0,1:T(8,128)(2,1)}, u32[]{:S(2)}) copy-start(bf16[2048,64]{0,1:T(8,128)(2,1)} %param.16) | copy-start | bytes 786436
  106.8 304.1 %copy-start.3 = (bf16[1,256,64]{1,2,0:T(8,128)(2,1)S(1)}, bf16[1,256,64]{1,2,0:T(8,128)(2,1)}, u32[]{:S(2)}) copy-start(bf16[1,256,64]{1,2,0:T(8,128)(2,1)} %param.15) | copy-start | bytes 98308
  110.2 757.2 %all-gather.6.cloned.1.call-start = ((), (), s32[]{:S(2)}) async-start(), calls=%async_computation.1 | async-start | bytes 2129920 | tf_op jit(solution)/shard_map/all_gather | solution.py:116
  568.7 301.0 %copy-start.1 = (bf16[128,4096]{1,0:T(8,128)(2,1)S(1)}, bf16[128,4096]{1,0:T(8,128)(2,1)}, u32[]{:S(2)}) copy-start(bf16[128,4096]{1,0:T(8,128)(2,1)} %param.19) | copy-start | bytes 3145732
  568.7 630.3 %reduce-scatter.2.cloned.1.call-start = ((), (), s32[]{:S(2)}) async-start(), calls=%async_computation.2 | async-start | bytes 4259840 | tf_op jit(solution)/shard_map/reduce_scatter | solution.py:122
  872.4 0.7 copy-start.4
Sparse Core Ops, SparseCore 0:
  9.5 76.3 all-gather.7
  110.3 299.0 all-gather.9
  568.8 298.5 all-gather.5
  872.6 326.3 reduce-scatter.1
where the time goes:
time: 1210 us
  waiting for transfers between devices  1000 us (83%)
  blocking collectives  157 us (13%)
  local copies, waits for them, and re-layouts  19.5 us (2%)
  between operations  13.3 us (1%)
  matrix products  13 us (1%)
    reduce_scatter x1, waiting for transfers between devices, body(): lax.psum_scatter(partial_value, 'req', scatter_dimension=1, tiled=True)  326 us
    all_gather x1, waiting for transfers between devices, body(): lax.all_gather(attention, 'req', axis=0, tiled=True)  299 us
    all_gather x1, waiting for transfers between devices, body(): lax.all_gather(normed, 'req', axis=1, tiled=True)  299 us
    psum x1, blocking collectives, body(): row_sumsq = lax.psum(partial_sq, 'req')  157 us
    all_gather x1, waiting for transfers between devices, body(): lax.all_gather(own_pool, 'grp', axis=0, tiled=True)  76.7 us
  transfers between devices with their start and end apart: 4, of which 4 were waited for; matrix products, arithmetic and copies ran while one was open for 0% of the time, Pallas kernels for 0%

commit v1 on v0

--- a/solution.py
+++ b/solution.py
@@ -74,6 +74,11 @@
     return ordered.reshape(row_count, QH * HD).astype(jnp.bfloat16)
 
 
+def gather_rows(block, count):
+    spread = jnp.broadcast_to(block[None], (count,) + block.shape)
+    return lax.all_to_all(spread, "req", 0, 0, tiled=False)
+
+
 def body(
     queries,
     suffix_kv,
@@ -98,28 +103,37 @@
         table_row,
     )
     attention = with_suffix(softmax_state, own_heads, suffix_kv[0, 0])
+    req_count = lax.psum(1, "req")
     projected = jnp.dot(
-        lax.all_gather(attention, "req", axis=0, tiled=True),
+        gather_rows(attention, req_count).reshape(-1, attention.shape[-1]),
         out_weight,
         preferred_element_type=jnp.float32,
     )
     stream = (residual[0].astype(jnp.float32) + projected).astype(jnp.bfloat16)
     wide_local = stream.astype(jnp.float32)
-    partial_sq = jnp.sum(wide_local * wide_local, axis=1)
-    row_sumsq = lax.psum(partial_sq, "req")
+    token_count, local_width = stream.shape
+    with_gain = jnp.concatenate([stream, norm_gain.reshape(1, local_width)], axis=0)
+    gathered = gather_rows(with_gain, req_count)
+    full_stream = jnp.transpose(gathered[:, :token_count], (1, 0, 2)).reshape(token_count, -1)
+    full_gain = gathered[:, token_count].reshape(-1)
+    wide = full_stream.astype(jnp.float32)
+    row_sumsq = jnp.sum(wide * wide, axis=1)
     inverse_rms = lax.rsqrt(row_sumsq / D + 1e-05)
-    normed = (wide_local * inverse_rms[:, None] * norm_gain.astype(jnp.float32)[None, :]).astype(
+    normed = (wide * inverse_rms[:, None] * full_gain.astype(jnp.float32)[None, :]).astype(
         jnp.bfloat16
     )
     gate_up_out = jnp.einsum(
         "nc,kcf->knf",
-        lax.all_gather(normed, "req", axis=1, tiled=True),
+        normed,
         gate_up,
         preferred_element_type=jnp.float32,
     )
     hidden = (jax.nn.silu(gate_up_out[0]) * gate_up_out[1]).astype(jnp.bfloat16)
     partial_value = jnp.dot(hidden, down_weight, preferred_element_type=jnp.float32)
-    summed = lax.psum_scatter(partial_value, "req", scatter_dimension=1, tiled=True)
+    blocks = jnp.transpose(
+        partial_value.reshape(token_count, req_count, local_width), (1, 0, 2)
+    )
+    summed = jnp.sum(lax.all_to_all(blocks, "req", 0, 0, tiled=False), axis=0)
     lengths = suffix_len[0]
     slot_index = jnp.arange(stream.shape[0], dtype=jnp.int32) % slot_count
     slot_live = (slot_index < jnp.repeat(lengths, slot_count)).astype(jnp.float32)

time: 1210 us -> 358 us (0.30)
  the two profiles are of different devices: /device:TPU:128 before, /device:TPU:8 now
where the time goes in v1:
time: 358 us; the launch traced here: 357 us
  waiting for transfers between devices  272 us (76%)
  local copies, waits for them, and re-layouts  24.2 us (7%)
  starting transfers between devices  23.3 us (7%)
  between operations  13.6 us (4%)
  matrix products  12 us (3%)
  other arithmetic  11.6 us (3%)
    all_to_all x2, waiting for transfers between devices, gather_rows(): return lax.all_to_all(spread, 'req', 0, 0, tiled=False)  100 us
    all_to_all x1, waiting for transfers between devices, body(): summed = jnp.sum(lax.all_to_all(blocks, 'req', 0, 0, tiled=False), axis=0)  93.1 us
    all_gather x1, waiting for transfers between devices, body(): lax.all_gather(own_pool, 'grp', axis=0, tiled=True)  78.4 us
    all_to_all x2, starting transfers between devices, gather_rows(): return lax.all_to_all(spread, 'req', 0, 0, tiled=False)  16.7 us
  transfers between devices with their start and end apart: 4, of which 4 were waited for; matrix products, arithmetic and copies ran while one was open for 1% of the time, Pallas kernels for 0%

profile of v1, /device:TPU:8, one launch (start us, length us, event | category | flops | bytes accessed | tf_op | source)
XLA Modules:
  0.0 356.9 jit_solution(12086617339165512640)
XLA Ops:
  6.5 0.0 copy-start
  6.5 0.0 all-gather.3.cloned.1.call-start
  6.5 0.7 all-gather.3.cloned.1.call-update
  7.3 0.7 fusion.45
  8.0 0.1 broadcast_bitcast_fusion
  8.1 1.0 fusion.57
  9.1 78.4 %all-gather.3.cloned.1.call-done = bf16[1,1,24,2,128,512]{5,4,3,1,0,2:T(8,128)(2,1)} async-done(((bf16[1,1,3,2,128,512]{5,4,3,1,0,2:T(8,128)(2,1)}), bf16[1,1,24,2,128,512]{5,4,3,1,0,2:T(8,128)(2,1)}) %all-gather.3.cloned.1.call-update) | async-done | bytes 6291472 | tf_op jit(solution)/shard_map/all_gather | solution.py:101
  87.5 6.2 %fusion.55 = (bf16[24,1,128,512]{3,2,1,0:T(8,128)(2,1)}, bf16[24,1,128,512]{3,2,1,0:T(8,128)(2,1)}) fusion(bf16[24,2,128,512]{3,2,1,0:T(8,128)(2,1)} %bitcast.93), kind=kLoop, calls=%fused_computation.63 | loop fusion | bytes 12582912 | tf_op jit(solution)/shard_map/slice | solution.py:33
  93.7 0.0 copy-start.5
  93.7 5.5 %reshape.97 = bf16[3072,4,128]{2,1,0:T(4,128)(2,1)} reshape(bf16[24,1,128,512]{3,2,1,0:T(8,128)(2,1)} %get-tuple-element.8) | data formatting | bytes 6291456 | tf_op jit(solution)/shard_map/reshape;squeeze | solution.py:32
  99.2 0.0 copy-done.5
  99.2 2.9 fusion.56
  102.2 0.0 copy-done.6
  102.2 0.2 convolution_bitcast_fusion.1
  102.4 5.5 %reshape.98 = bf16[3072,4,128]{2,1,0:T(4,128)(2,1)} reshape(bf16[24,1,128,512]{3,2,1,0:T(8,128)(2,1)} %get-tuple-element.7) | data formatting | bytes 6291456 | tf_op jit(solution)/shard_map/reshape;squeeze | solution.py:33
  108.0 0.5 fusion.28
  108.5 0.0 copy-start.4
  108.5 2.8 fusion.25
  111.2 0.0 copy-start.1
  111.2 0.0 copy-start.2
  111.3 1.5 broadcast_in_dim.68
  112.8 10.5 %all-to-all-start = ((bf16[64,4,2048]{2,1,0:T(4,128)(2,1)}), bf16[64,4,2048]{2,1,0:T(4,128)(2,1)S(1)}, u32[]{:S(2)}, u32[]{:S(2)}) async-start(bf16[64,4,2048]{2,1,0:T(4,128)(2,1)} %broadcast_in_dim.68), calls=%async_computation | async-start | bytes 2097152 | tf_op jit(solution)/shard_map/all_to_all | solution.py:79
  123.3 0.0 copy-done.4
  123.3 0.1 copy.51
  123.4 29.0 %all-to-all-done = bf16[64,4,2048]{2,1,0:T(4,128)(2,1)S(1)} async-done(((bf16[64,4,2048]{2,1,0:T(4,128)(2,1)}), bf16[64,4,2048]{2,1,0:T(4,128)(2,1)S(1)}, u32[]{:S(2)}, u32[]{:S(2)}) %all-to-all-start) | async-done | bytes 1048608 | tf_op jit(solution)/shard_map/all_to_all | solution.py:79
  152.4 1.1 reshape.84
  153.5 0.0 copy-done.1
  153.5 0.0 copy-done.2
  153.5 1.7 fusion.11
  155.2 2.2 broadcast_in_dim.69
  157.4 6.2 %all-to-all-start.1 = ((bf16[64,257,64]{1,2,0:T(8,128)(2,1)}), bf16[64,257,64]{1,2,0:T(8,128)(2,1)}, u32[]{:S(2)}, u32[]{:S(2)}) async-start(bf16[64,257,64]{1,2,0:T(8,128)(2,1)} %broadcast_in_dim.69), calls=%async_computation.1 | async-start | bytes 6291456 | tf_op jit(solution)/shard_map/all_to_all | solution.py:79
  163.6 1.6 copy.53
  165.2 71.1 %all-to-all-done.1 = bf16[64,257,64]{1,2,0:T(8,128)(2,1)} async-done(((bf16[64,257,64]{1,2,0:T(8,128)(2,1)}), bf16[64,257,64]{1,2,0:T(8,128)(2,1)}, u32[]{:S(2)}, u32[]{:S(2)}) %all-to-all-start.1) | async-done | bytes 2105376 | tf_op jit(solution)/shard_map/all_to_all | solution.py:79
  236.4 2.2 multiply_reduce_fusion
  238.5 1.8 convert_reduce_fusion
  240.4 0.1 reshape.89
  240.5 2.1 slice_convert_fusion
  242.6 1.0 fusion.1
  243.6 0.0 copy-done
  243.6 0.8 fusion.8
  244.4 2.7 convolution_bitcast_fusion
  247.1 6.6 %all-to-all-start.2 = ((f32[64,256,64]{1,2,0:T(8,128)}), f32[64,256,64]{1,2,0:T(8,128)}, u32[]{:S(2)}, u32[]{:S(2)}) async-start(f32[64,256,64]{1,2,0:T(8,128)} %convolution_bitcast_fusion), calls=%async_computation.2 | async-start | bytes 8388608 | tf_op jit(solution)/shard_map/all_to_all | solution.py:136
  253.7 0.0 copy-done.3
  253.7 0.1 broadcast_in_dim.70
  253.8 0.1 reshape.86
  253.9 93.1 %all-to-all-done.2 = f32[64,256,64]{1,2,0:T(8,128)} async-done(((f32[64,256,64]{1,2,0:T(8,128)}), f32[64,256,64]{1,2,0:T(8,128)}, u32[]{:S(2)}, u32[]{:S(2)}) %all-to-all-start.2) | async-done | bytes 4194336 | tf_op jit(solution)/shard_map/all_to_all | solution.py:136
  347.0 2.4 reduce_sum.45
  349.4 0.6 fusion.37
  (9 shorter events, 0.1 us)
Async XLA Ops:
  6.5 237.1 %copy-start = (bf16[2,4096,128]{2,1,0:T(8,128)(2,1)S(1)}, bf16[2,4096,128]{2,1,0:T(8,128)(2,1)}, u32[]{:S(2)}) copy-start(bf16[2,4096,128]{2,1,0:T(8,128)(2,1)} %param.18) | copy-start | bytes 6291460
  6.5 80.9 %all-gather.3.cloned.1.call-start = ((), (), s32[]{:S(2)}) async-start(), calls=%async_computation.3 | async-start | bytes 7077888 | tf_op jit(solution)/shard_map/all_gather | solution.py:101
  93.7 5.5 %copy-start.5 = (bf16[1,1,4,2048]{3,2,1,0:T(4,128)(2,1)S(1)}, bf16[1,1,4,2048]{3,2,1,0:T(4,128)(2,1)}, u32[]{:S(2)}) copy-start(bf16[1,1,4,2048]{3,2,1,0:T(4,128)(2,1)} %param.10) | copy-start | bytes 49156
  99.2 3.0 copy-start.6
  108.5 14.8 %copy-start.4 = (bf16[64]{0:T(256)(128)(2,1)S(1)}, bf16[64]{0:T(256)(128)(2,1)}, u32[]{:S(2)}) copy-start(bf16[64]{0:T(256)(128)(2,1)} %param.17) | copy-start | bytes 388
  111.2 42.3 %copy-start.1 = (bf16[2048,64]{0,1:T(8,128)(2,1)S(1)}, bf16[2048,64]{0,1:T(8,128)(2,1)}, u32[]{:S(2)}) copy-start(bf16[2048,64]{0,1:T(8,128)(2,1)} %param.16) | copy-start | bytes 786436
  111.2 42.3 %copy-start.2 = (bf16[1,256,64]{1,2,0:T(8,128)(2,1)S(1)}, bf16[1,256,64]{1,2,0:T(8,128)(2,1)}, u32[]{:S(2)}) copy-start(bf16[1,256,64]{1,2,0:T(8,128)(2,1)} %param.15) | copy-start | bytes 98308
  112.8 39.6 %all-to-all-start = ((bf16[64,4,2048]{2,1,0:T(4,128)(2,1)}), bf16[64,4,2048]{2,1,0:T(4,128)(2,1)S(1)}, u32[]{:S(2)}, u32[]{:S(2)}) async-start(bf16[64,4,2048]{2,1,0:T(4,128)(2,1)} %broadcast_in_dim.68), calls=%async_computation | async-start | bytes 2097152 | tf_op jit(solution)/shard_map/all_to_all | solution.py:79
  157.4 78.9 %all-to-all-start.1 = ((bf16[64,257,64]{1,2,0:T(8,128)(2,1)}), bf16[64,257,64]{1,2,0:T(8,128)(2,1)}, u32[]{:S(2)}, u32[]{:S(2)}) async-start(bf16[64,257,64]{1,2,0:T(8,128)(2,1)} %broadcast_in_dim.69), calls=%async_computation.1 | async-start | bytes 6291456 | tf_op jit(solution)/shard_map/all_to_all | solution.py:79
  247.1 6.6 %copy-start.3 = (s32[1,64]{1,0:T(1,128)S(1)}, s32[1,64]{1,0:T(1,128)}, u32[]{:S(2)}) copy-start(s32[1,64]{1,0:T(1,128)} %param.14) | copy-start | bytes 772
  247.1 99.9 %all-to-all-start.2 = ((f32[64,256,64]{1,2,0:T(8,128)}), f32[64,256,64]{1,2,0:T(8,128)}, u32[]{:S(2)}, u32[]{:S(2)}) async-start(f32[64,256,64]{1,2,0:T(8,128)} %convolution_bitcast_fusion), calls=%async_computation.2 | async-start | bytes 8388608 | tf_op jit(solution)/shard_map/all_to_all | solution.py:136
Sparse Core Ops, SparseCore 0:
  9.5 77.9 all-gather.2

commit v2 on v1

v2 whole, which is shorter than its diff:
```python
import jax
import jax.numpy as jnp
from jax import lax
from jax.sharding import PartitionSpec as P

D = 4096
HD = 128
QH = 16
KVH = 4
PAGE = 128


def heads_of(rows):
    row_count = rows.shape[0]
    return jnp.transpose(rows.reshape(row_count, KVH, QH // KVH, HD), (1, 2, 0, 3))


def attend(own_queries, own_suffix, own_pool, table_row):
    slot_count = own_queries.shape[0]
    member_count = lax.psum(1, "grp")
    member = lax.axis_index("grp")
    pool_pages = own_pool.shape[0]
    spread = jnp.broadcast_to(own_queries[None], (member_count,) + own_queries.shape)
    all_queries = lax.all_to_all(spread, "grp", 0, 0, tiled=False)
    query_heads = heads_of(all_queries.reshape(member_count * slot_count, -1))
    page_ids = member * pool_pages + jnp.arange(pool_pages, dtype=jnp.int32)
    page_used = jnp.any(page_ids[:, None] == table_row[None, :], axis=1)
    token_live = jnp.repeat(page_used, PAGE)
    key_rows = own_pool[:, 0].reshape(pool_pages * PAGE, KVH, HD)
    value_rows = own_pool[:, 1].reshape(pool_pages * PAGE, KVH, HD)
    scores = jnp.einsum(
        "jgsd,tjd->jgst", query_heads, key_rows, preferred_element_type=jnp.float32
    ) * HD ** (-0.5)
    scores = jnp.where(token_live, scores, -1e30)
    local_max = jnp.max(scores, axis=-1)
    weights = jnp.where(token_live, jnp.exp(scores - local_max[..., None]), 0.0)
    local_sum = jnp.sum(weights, axis=-1)
    weighted = jnp.einsum(
        "jgst,tjd->jgsd",
        weights.astype(jnp.bfloat16),
        value_rows,
        preferred_element_type=jnp.float32,
    )
    packed = jnp.concatenate([weighted, local_max[..., None], local_sum[..., None]], axis=-1)
    packed = packed.reshape(KVH, QH // KVH, member_count, slot_count, HD + 2)
    packed = jnp.transpose(packed, (2, 0, 1, 3, 4))
    parts = lax.all_to_all(packed, "grp", 0, 0, tiled=False)
    part_acc = parts[..., :HD]
    part_max = parts[..., HD]
    part_sum = parts[..., HD + 1]
    own_heads = heads_of(own_queries)
    suffix_keys = own_suffix[0].reshape(slot_count, KVH, HD)
    suffix_values = own_suffix[1].reshape(slot_count, KVH, HD)
    suffix_scores = jnp.einsum(
        "jgsd,tjd->jgst", own_heads, suffix_keys, preferred_element_type=jnp.float32
    ) * HD ** (-0.5)
    causal = jnp.arange(slot_count)[:, None] >= jnp.arange(slot_count)[None, :]
    suffix_scores = jnp.where(causal, suffix_scores, -1e30)
    merged_max = jnp.maximum(jnp.max(part_max, axis=0), jnp.max(suffix_scores, axis=-1))
    rescale = jnp.exp(part_max - merged_max[None])
    suffix_weights = jnp.where(causal, jnp.exp(suffix_scores - merged_max[..., None]), 0.0)
    total = jnp.sum(part_sum * rescale, axis=0) + jnp.sum(suffix_weights, axis=-1)
    accumulated = jnp.sum(part_acc * rescale[..., None], axis=0) + jnp.einsum(
        "jgst,tjd->jgsd",
        suffix_weights.astype(jnp.bfloat16),
        suffix_values,
        preferred_element_type=jnp.float32,
    )
    accumulated = accumulated / total[..., None]
    ordered = jnp.transpose(accumulated, (2, 0, 1, 3))
    return ordered.reshape(slot_count, QH * HD).astype(jnp.bfloat16)


def gather_rows(block, count):
    spread = jnp.broadcast_to(block[None], (count,) + block.shape)
    return lax.all_to_all(spread, "req", 0, 0, tiled=False)


def body(
    queries,
    suffix_kv,
    prefix_pool,
    page_table,
    suffix_len,
    residual,
    out_weight,
    norm_gain,
    gate_up,
    down_weight,
):
    slot_count = queries.shape[2]
    attention = attend(queries[0, 0], suffix_kv[0, 0], prefix_pool[0, 0], page_table[0])
    req_count = lax.psum(1, "req")
    projected = jnp.dot(
        gather_rows(attention, req_count).reshape(-1, attention.shape[-1]),
        out_weight,
        preferred_element_type=jnp.float32,
    )
    stream = (residual[0].astype(jnp.float32) + projected).astype(jnp.bfloat16)
    wide_local = stream.astype(jnp.float32)
    token_count, local_width = stream.shape
    with_gain = jnp.concatenate([stream, norm_gain.reshape(1, local_width)], axis=0)
    gathered = gather_rows(with_gain, req_count)
    full_stream = jnp.transpose(gathered[:, :token_count], (1, 0, 2)).reshape(token_count, -1)
    full_gain = gathered[:, token_count].reshape(-1)
    wide = full_stream.astype(jnp.float32)
    row_sumsq = jnp.sum(wide * wide, axis=1)
    inverse_rms = lax.rsqrt(row_sumsq / D + 1e-05)
    normed = (wide * inverse_rms[:, None] * full_gain.astype(jnp.float32)[None, :]).astype(
        jnp.bfloat16
    )
    gate_up_out = jnp.einsum(
        "nc,kcf->knf",
        normed,
        gate_up,
        preferred_element_type=jnp.float32,
    )
    hidden = (jax.nn.silu(gate_up_out[0]) * gate_up_out[1]).astype(jnp.bfloat16)
    partial_value = jnp.dot(hidden, down_weight, preferred_element_type=jnp.float32)
    blocks = jnp.transpose(
        partial_value.reshape(token_count, req_count, local_width), (1, 0, 2)
    )
    arrived = lax.all_to_all(blocks.astype(jnp.bfloat16), "req", 0, 0, tiled=False)
    summed = jnp.sum(arrived.astype(jnp.float32), axis=0)
    lengths = suffix_len[0]
    slot_index = jnp.arange(stream.shape[0], dtype=jnp.int32) % slot_count
    slot_live = (slot_index < jnp.repeat(lengths, slot_count)).astype(jnp.float32)
    result_rows = (wide_local + summed) * slot_live[:, None]
    return result_rows.astype(jnp.bfloat16)[None]


def solution(mesh):
    return jax.shard_map(
        body,
        mesh=mesh,
        in_specs=(
            P("grp", "req", None, None),
            P("grp", "req", None, None, None),
            P("grp", "req", None, None, None, None),
            P("req", None),
            P("grp", None),
            P("grp", None, "req"),
            P(None, "req"),
            P("req"),
            P(None, None, "req"),
            P("req", None),
        ),
        out_specs=P("grp", None, "req"),
        check_vma=False,
    )
```

time: 358 us -> 243 us (0.68)
  waiting for transfers between devices: 272 us -> 171 us
  starting transfers between devices: 23.3 us -> 37.9 us
  between operations: 13.6 us -> 0.27 us
  local copies, waits for them, and re-layouts: 24.2 us -> 13.7 us
  matrix products: 12 us -> 6.65 us
    all_gather x1 -> x0, waiting for transfers between devices: 78.4 us -> none  [body(): lax.all_gather(own_pool, 'grp', axis=0, tiled=True)]
    all_to_all x1 -> x3, waiting for transfers between devices: 93.1 us -> 73.8 us  [the longest x1 49.5 us: body(): lax.all_to_all(blocks.astype(jnp.bfloat16), 'req', 0, 0, tiled=False)]
    all_to_all x1 -> x3, starting transfers between devices: 6.57 us -> 20.7 us  [the longest x1 10.3 us: attend(): all_queries = lax.all_to_all(spread, 'grp', 0, 0, tiled=False)]
    another operation x2 -> x3, local copies, waits for them, and re-layouts: 11.1 us -> 1.01 us  [the longest x1 0.83 us: attend(): value_rows = own_pool[:, 1].reshape(pool_pages * PAGE, KVH, HD)]
    dot_general x4, matrix products: 6.87 us -> 2.2 us  [the longest x1 1.32 us: attend(): jnp.einsum('jgst,tjd->jgsd', weights.astype(jnp.bfloat16), value_rows, pr...]
    slice x1 -> x2, local copies, waits for them, and re-layouts: 6.21 us -> 1.65 us  [the longest x1 1.17 us: attend(): value_rows = own_pool[:, 1].reshape(pool_pages * PAGE, KVH, HD)]
  transfers between devices with their start and end apart: 4 -> 5, of which waited for: 4 -> 5; matrix products, arithmetic and copies ran while one was open for 1% -> 2% of each run, Pallas kernels for 0% -> 0%
where the time goes in v2:
time: 243 us; the launch traced here: 242 us
  waiting for transfers between devices  171 us (70%)
  starting transfers between devices  37.9 us (16%)
  local copies, waits for them, and re-layouts  13.7 us (6%)
  other arithmetic  12.7 us (5%)
  matrix products  6.65 us (3%)
    all_to_all x2, waiting for transfers between devices, gather_rows(): return lax.all_to_all(spread, 'req', 0, 0, tiled=False)  97.1 us
    all_to_all x1, waiting for transfers between devices, body(): lax.all_to_all(blocks.astype(jnp.bfloat16), 'req', 0, 0, tiled=False)  49.5 us
    all_to_all x1, waiting for transfers between devices, attend(): parts = lax.all_to_all(packed, 'grp', 0, 0, tiled=False)  17.5 us
    all_to_all x2, starting transfers between devices, gather_rows(): return lax.all_to_all(spread, 'req', 0, 0, tiled=False)  17.2 us
    all_to_all x1, starting transfers between devices, attend(): all_queries = lax.all_to_all(spread, 'grp', 0, 0, tiled=False)  10.3 us
    all_to_all x1, starting transfers between devices, body(): lax.all_to_all(blocks.astype(jnp.bfloat16), 'req', 0, 0, tiled=False)  6.88 us
    all_to_all x1, waiting for transfers between devices, attend(): all_queries = lax.all_to_all(spread, 'grp', 0, 0, tiled=False)  6.88 us
  transfers between devices with their start and end apart: 5, of which 5 were waited for; matrix products, arithmetic and copies ran while one was open for 2% of the time, Pallas kernels for 0%

profile of v2, /device:TPU:8, one launch (start us, length us, event | category | flops | bytes accessed | tf_op | source)
XLA Modules:
  0.0 242.2 jit_solution(8276006520883429530)
XLA Ops:
  0.0 1.6 broadcast_in_dim.70
  1.6 10.3 %all-to-all-start = ((bf16[8,4,2048]{2,1,0:T(4,128)(2,1)}), bf16[8,4,2048]{2,1,0:T(4,128)(2,1)S(1)}, u32[]{:S(2)}, u32[]{:S(2)}) async-start(bf16[8,4,2048]{2,1,0:T(4,128)(2,1)} %broadcast_in_dim.70), calls=%async_computation | async-start | bytes 262144 | tf_op jit(solution)/shard_map/all_to_all | solution.py:24
  11.9 1.2 fusion.45
  13.0 0.8 compare_reduce_fusion
  13.9 0.1 reshape_squeeze.16
  14.0 0.8 reshape_squeeze.17
  14.9 6.9 %all-to-all-done = bf16[8,4,2048]{2,1,0:T(4,128)(2,1)S(1)} async-done(((bf16[8,4,2048]{2,1,0:T(4,128)(2,1)}), bf16[8,4,2048]{2,1,0:T(4,128)(2,1)S(1)}, u32[]{:S(2)}, u32[]{:S(2)}) %all-to-all-start) | async-done | bytes 131104 | tf_op jit(solution)/shard_map/all_to_all | solution.py:24
  21.8 0.1 reshape_reshape.3
  21.9 0.4 fusion.47
  22.3 0.1 concatenate.14
  22.4 0.3 fusion.13
  22.7 1.3 fusion.15
  24.0 0.1 concatenate.15
  24.1 0.9 copy.62
  25.0 0.9 copy.61
  25.9 1.0 maximum_bitcast_fusion
  26.9 3.5 %all-to-all-start.1 = ((f32[8,4,4,4,130]{4,3,2,1,0:T(4,128)}), f32[8,4,4,4,130]{4,3,2,1,0:T(4,128)S(1)}, u32[]{:S(2)}, u32[]{:S(2)}) async-start(f32[8,4,4,4,130]{4,3,2,1,0:T(4,128)} %maximum_bitcast_fusion), calls=%async_computation.1 | async-start | bytes 1048576 | tf_op jit(solution)/shard_map/all_to_all | solution.py:47
  30.5 0.3 fusion.48
  30.7 17.5 %all-to-all-done.1 = f32[8,4,4,4,130]{4,3,2,1,0:T(4,128)S(1)} async-done(((f32[8,4,4,4,130]{4,3,2,1,0:T(4,128)}), f32[8,4,4,4,130]{4,3,2,1,0:T(4,128)S(1)}, u32[]{:S(2)}, u32[]{:S(2)}) %all-to-all-start.1) | async-done | bytes 266272 | tf_op jit(solution)/shard_map/all_to_all | solution.py:47
  48.2 0.3 fusion.46
  48.5 0.5 copy.85
  49.0 0.5 copy.69
  49.4 0.1 exponential_bitcast_fusion
  49.6 0.2 fusion.31
  49.8 0.2 copy.65
  50.0 0.2 fusion.22
  50.2 0.2 fusion.12
  50.4 1.5 broadcast_in_dim.76
  51.9 11.1 %all-to-all-start.2 = ((bf16[64,4,2048]{2,1,0:T(4,128)(2,1)}), bf16[64,4,2048]{2,1,0:T(4,128)(2,1)S(1)}, u32[]{:S(2)}, u32[]{:S(2)}) async-start(bf16[64,4,2048]{2,1,0:T(4,128)(2,1)} %broadcast_in_dim.76), calls=%async_computation.2 | async-start | bytes 2097152 | tf_op jit(solution)/shard_map/all_to_all | solution.py:76
  63.1 0.1 copy.70
  63.2 27.3 %all-to-all-done.2 = bf16[64,4,2048]{2,1,0:T(4,128)(2,1)S(1)} async-done(((bf16[64,4,2048]{2,1,0:T(4,128)(2,1)}), bf16[64,4,2048]{2,1,0:T(4,128)(2,1)S(1)}, u32[]{:S(2)}, u32[]{:S(2)}) %all-to-all-start.2) | async-done | bytes 1048608 | tf_op jit(solution)/shard_map/all_to_all | solution.py:76
  90.5 1.1 reshape.87
  91.7 1.7 fusion.8
  93.3 2.2 broadcast_in_dim.77
  95.5 6.1 %all-to-all-start.3 = ((bf16[64,257,64]{1,2,0:T(8,128)(2,1)}), bf16[64,257,64]{1,2,0:T(8,128)(2,1)}, u32[]{:S(2)}, u32[]{:S(2)}) async-start(bf16[64,257,64]{1,2,0:T(8,128)(2,1)} %broadcast_in_dim.77), calls=%async_computation.3 | async-start | bytes 6291456 | tf_op jit(solution)/shard_map/all_to_all | solution.py:76
  101.6 1.6 copy.72
  103.2 69.7 %all-to-all-done.3 = bf16[64,257,64]{1,2,0:T(8,128)(2,1)} async-done(((bf16[64,257,64]{1,2,0:T(8,128)(2,1)}), bf16[64,257,64]{1,2,0:T(8,128)(2,1)}, u32[]{:S(2)}, u32[]{:S(2)}) %all-to-all-start.3) | async-done | bytes 2105376 | tf_op jit(solution)/shard_map/all_to_all | solution.py:76
  173.0 1.8 convert_reduce_fusion.1
  174.9 2.2 multiply_reduce_fusion
  177.1 2.1 slice_convert_fusion
  179.2 1.0 fusion.1
  180.2 0.8 fusion.5
  181.0 2.0 convert_bitcast_fusion
  183.1 6.9 %all-to-all-start.4 = ((bf16[64,256,64]{1,2,0:T(8,128)(2,1)}), bf16[64,256,64]{1,2,0:T(8,128)(2,1)}, u32[]{:S(2)}, u32[]{:S(2)}) async-start(bf16[64,256,64]{1,2,0:T(8,128)(2,1)} %convert_bitcast_fusion), calls=%async_computation.4 | async-start | bytes 4194304 | tf_op jit(solution)/shard_map/all_to_all | solution.py:123
  190.0 0.1 reshape.89
  190.2 49.5 %all-to-all-done.4 = bf16[64,256,64]{1,2,0:T(8,128)(2,1)} async-done(((bf16[64,256,64]{1,2,0:T(8,128)(2,1)}), bf16[64,256,64]{1,2,0:T(8,128)(2,1)}, u32[]{:S(2)}, u32[]{:S(2)}) %all-to-all-start.4) | async-done | bytes 2097184 | tf_op jit(solution)/shard_map/all_to_all | solution.py:123
  239.6 1.9 convert_reduce_fusion
  241.5 0.6 fusion.28
  (25 shorter events, 0.3 us)
Async XLA Ops:
  0.0 180.2 %copy-start = (bf16[2,4096,128]{2,1,0:T(8,128)(2,1)S(1)}, bf16[2,4096,128]{2,1,0:T(8,128)(2,1)}, u32[]{:S(2)}) copy-start(bf16[2,4096,128]{2,1,0:T(8,128)(2,1)} %param.18) | copy-start | bytes 6291460
  1.6 20.2 %all-to-all-start = ((bf16[8,4,2048]{2,1,0:T(4,128)(2,1)}), bf16[8,4,2048]{2,1,0:T(4,128)(2,1)S(1)}, u32[]{:S(2)}, u32[]{:S(2)}) async-start(bf16[8,4,2048]{2,1,0:T(4,128)(2,1)} %broadcast_in_dim.70), calls=%async_computation | async-start | bytes 262144 | tf_op jit(solution)/shard_map/all_to_all | solution.py:24
  21.9 8.6 %copy-start.3 = (bf16[1,1,4,2048]{3,2,1,0:T(4,128)(2,1)S(1)}, bf16[1,1,4,2048]{3,2,1,0:T(4,128)(2,1)}, u32[]{:S(2)}) copy-start(bf16[1,1,4,2048]{3,2,1,0:T(4,128)(2,1)} %param.10) | copy-start | bytes 49156
  21.9 8.6 %copy-start.6 = (bf16[1,1,2,4,512]{4,3,2,1,0:T(4,128)(2,1)S(1)}, bf16[1,1,2,4,512]{4,3,2,1,0:T(4,128)(2,1)}, u32[]{:S(2)}) copy-start(bf16[1,1,2,4,512]{4,3,2,1,0:T(4,128)(2,1)} %param.11) | copy-start | bytes 24580
  26.9 21.3 %all-to-all-start.1 = ((f32[8,4,4,4,130]{4,3,2,1,0:T(4,128)}), f32[8,4,4,4,130]{4,3,2,1,0:T(4,128)S(1)}, u32[]{:S(2)}, u32[]{:S(2)}) async-start(f32[8,4,4,4,130]{4,3,2,1,0:T(4,128)} %maximum_bitcast_fusion), calls=%async_computation.1 | async-start | bytes 1048576 | tf_op jit(solution)/shard_map/all_to_all | solution.py:47
  30.4 32.7 %copy-start.5 = (bf16[64]{0:T(256)(128)(2,1)S(1)}, bf16[64]{0:T(256)(128)(2,1)}, u32[]{:S(2)}) copy-start(bf16[64]{0:T(256)(128)(2,1)} %param.17) | copy-start | bytes 388
  49.5 42.1 %copy-start.1 = (bf16[2048,64]{0,1:T(8,128)(2,1)S(1)}, bf16[2048,64]{0,1:T(8,128)(2,1)}, u32[]{:S(2)}) copy-start(bf16[2048,64]{0,1:T(8,128)(2,1)} %param.16) | copy-start | bytes 786436
  49.6 42.1 %copy-start.2 = (bf16[1,256,64]{1,2,0:T(8,128)(2,1)S(1)}, bf16[1,256,64]{1,2,0:T(8,128)(2,1)}, u32[]{:S(2)}) copy-start(bf16[1,256,64]{1,2,0:T(8,128)(2,1)} %param.15) | copy-start | bytes 98308
  51.9 38.6 %all-to-all-start.2 = ((bf16[64,4,2048]{2,1,0:T(4,128)(2,1)}), bf16[64,4,2048]{2,1,0:T(4,128)(2,1)S(1)}, u32[]{:S(2)}, u32[]{:S(2)}) async-start(bf16[64,4,2048]{2,1,0:T(4,128)(2,1)} %broadcast_in_dim.76), calls=%async_computation.2 | async-start | bytes 2097152 | tf_op jit(solution)/shard_map/all_to_all | solution.py:76
  95.5 77.4 %all-to-all-start.3 = ((bf16[64,257,64]{1,2,0:T(8,128)(2,1)}), bf16[64,257,64]{1,2,0:T(8,128)(2,1)}, u32[]{:S(2)}, u32[]{:S(2)}) async-start(bf16[64,257,64]{1,2,0:T(8,128)(2,1)} %broadcast_in_dim.77), calls=%async_computation.3 | async-start | bytes 6291456 | tf_op jit(solution)/shard_map/all_to_all | solution.py:76
  181.0 8.9 %copy-start.4 = (s32[1,64]{1,0:T(1,128)S(1)}, s32[1,64]{1,0:T(1,128)}, u32[]{:S(2)}) copy-start(s32[1,64]{1,0:T(1,128)} %param.14) | copy-start | bytes 772
  183.1 56.6 %all-to-all-start.4 = ((bf16[64,256,64]{1,2,0:T(8,128)(2,1)}), bf16[64,256,64]{1,2,0:T(8,128)(2,1)}, u32[]{:S(2)}, u32[]{:S(2)}) async-start(bf16[64,256,64]{1,2,0:T(8,128)(2,1)} %convert_bitcast_fusion), calls=%async_computation.4 | async-start | bytes 4194304 | tf_op jit(solution)/shard_map/all_to_all | solution.py:123

commit v3 on v2

--- a/solution.py
+++ b/solution.py
@@ -89,8 +89,9 @@
     down_weight,
 ):
     slot_count = queries.shape[2]
+    req_count = lax.psum(1, "req")
+    full_gain = gather_rows(norm_gain, req_count).reshape(-1)
     attention = attend(queries[0, 0], suffix_kv[0, 0], prefix_pool[0, 0], page_table[0])
-    req_count = lax.psum(1, "req")
     projected = jnp.dot(
         gather_rows(attention, req_count).reshape(-1, attention.shape[-1]),
         out_weight,
@@ -99,10 +100,8 @@
     stream = (residual[0].astype(jnp.float32) + projected).astype(jnp.bfloat16)
     wide_local = stream.astype(jnp.float32)
     token_count, local_width = stream.shape
-    with_gain = jnp.concatenate([stream, norm_gain.reshape(1, local_width)], axis=0)
-    gathered = gather_rows(with_gain, req_count)
-    full_stream = jnp.transpose(gathered[:, :token_count], (1, 0, 2)).reshape(token_count, -1)
-    full_gain = gathered[:, token_count].reshape(-1)
+    gathered = gather_rows(stream, req_count)
+    full_stream = jnp.transpose(gathered, (1, 0, 2)).reshape(token_count, -1)
     wide = full_stream.astype(jnp.float32)
     row_sumsq = jnp.sum(wide * wide, axis=1)
     inverse_rms = lax.rsqrt(row_sumsq / D + 1e-05)

time: 243 us -> 228 us (0.938)
  waiting for transfers between devices: 171 us -> 125 us
  blocking collectives: 0 us -> 38.5 us
  starting transfers between devices: 37.9 us -> 32.9 us
  other arithmetic: 12.7 us -> 9.76 us
    all_to_all x2, waiting for transfers between devices: 97.1 us -> 52.8 us  [gather_rows(): return lax.all_to_all(spread, 'req', 0, 0, tiled=False)]
    all_to_all x0 -> x1, blocking collectives: none -> 38.5 us  [gather_rows(): return lax.all_to_all(spread, 'req', 0, 0, tiled=False)]
    all_to_all x2, starting transfers between devices: 17.2 us -> 12.3 us  [gather_rows(): return lax.all_to_all(spread, 'req', 0, 0, tiled=False)]
  transfers between devices with their start and end apart: 5 -> 5, of which waited for: 5 -> 5; matrix products, arithmetic and copies ran while one was open for 2% -> 4% of each run, Pallas kernels for 0% -> 0%
where the time goes in v3:
time: 228 us
  waiting for transfers between devices  125 us (55%)
  blocking collectives  38.5 us (17%)
  starting transfers between devices  32.9 us (14%)
  local copies, waits for them, and re-layouts  14.1 us (6%)
  other arithmetic  9.76 us (4%)
  matrix products  6.65 us (3%)
    all_to_all x2, waiting for transfers between devices, gather_rows(): return lax.all_to_all(spread, 'req', 0, 0, tiled=False)  52.8 us
    all_to_all x1, waiting for transfers between devices, body(): lax.all_to_all(blocks.astype(jnp.bfloat16), 'req', 0, 0, tiled=False)  48.3 us
    all_to_all x1, blocking collectives, gather_rows(): return lax.all_to_all(spread, 'req', 0, 0, tiled=False)  38.5 us
    all_to_all x1, waiting for transfers between devices, attend(): parts = lax.all_to_all(packed, 'grp', 0, 0, tiled=False)  17.5 us
    all_to_all x2, starting transfers between devices, gather_rows(): return lax.all_to_all(spread, 'req', 0, 0, tiled=False)  12.3 us
    all_to_all x1, starting transfers between devices, attend(): all_queries = lax.all_to_all(spread, 'grp', 0, 0, tiled=False)  10.3 us
    all_to_all x1, waiting for transfers between devices, attend(): all_queries = lax.all_to_all(spread, 'grp', 0, 0, tiled=False)  6.88 us
    all_to_all x1, starting transfers between devices, body(): lax.all_to_all(blocks.astype(jnp.bfloat16), 'req', 0, 0, tiled=False)  6.81 us
  transfers between devices with their start and end apart: 5, of which 5 were waited for; matrix products, arithmetic and copies ran while one was open for 4% of the time, Pallas kernels for 0%

profile of v3, /device:TPU:8, one launch (start us, length us, event | category | flops | bytes accessed | tf_op | source)
XLA Modules:
  0.0 227.5 jit_solution(7105502296811103362)
XLA Ops:
  0.0 1.6 broadcast_in_dim.76
  1.6 10.3 %all-to-all-start = ((bf16[8,4,2048]{2,1,0:T(4,128)(2,1)}), bf16[8,4,2048]{2,1,0:T(4,128)(2,1)S(1)}, u32[]{:S(2)}, u32[]{:S(2)}) async-start(bf16[8,4,2048]{2,1,0:T(4,128)(2,1)} %broadcast_in_dim.76), calls=%async_computation | async-start | bytes 262144 | tf_op jit(solution)/shard_map/all_to_all | solution.py:24
  11.9 1.2 fusion.45
  13.0 0.8 compare_reduce_fusion
  13.9 0.1 reshape_squeeze.15
  14.0 0.8 reshape_squeeze.16
  14.9 6.9 %all-to-all-done = bf16[8,4,2048]{2,1,0:T(4,128)(2,1)S(1)} async-done(((bf16[8,4,2048]{2,1,0:T(4,128)(2,1)}), bf16[8,4,2048]{2,1,0:T(4,128)(2,1)S(1)}, u32[]{:S(2)}, u32[]{:S(2)}) %all-to-all-start) | async-done | bytes 131104 | tf_op jit(solution)/shard_map/all_to_all | solution.py:24
  21.8 0.1 reshape_reshape.3
  21.9 0.4 fusion.47
  22.3 0.7 concatenate.11
  23.0 0.3 fusion.13
  23.3 1.3 fusion.15
  24.6 0.1 concatenate.12
  24.7 0.9 copy.48
  25.6 1.7 copy.47
  27.3 1.0 maximum_bitcast_fusion
  28.4 3.5 %all-to-all-start.1 = ((f32[8,4,4,4,130]{4,3,2,1,0:T(4,128)}), f32[8,4,4,4,130]{4,3,2,1,0:T(4,128)S(1)}, u32[]{:S(2)}, u32[]{:S(2)}) async-start(f32[8,4,4,4,130]{4,3,2,1,0:T(4,128)} %maximum_bitcast_fusion), calls=%async_computation.1 | async-start | bytes 1048576 | tf_op jit(solution)/shard_map/all_to_all | solution.py:47
  31.9 0.3 fusion.48
  32.2 17.5 %all-to-all-done.1 = f32[8,4,4,4,130]{4,3,2,1,0:T(4,128)S(1)} async-done(((f32[8,4,4,4,130]{4,3,2,1,0:T(4,128)}), f32[8,4,4,4,130]{4,3,2,1,0:T(4,128)S(1)}, u32[]{:S(2)}, u32[]{:S(2)}) %all-to-all-start.1) | async-done | bytes 266272 | tf_op jit(solution)/shard_map/all_to_all | solution.py:47
  49.7 0.3 fusion.46
  49.9 0.5 copy.70
  50.4 0.5 copy.55
  50.9 0.1 exponential_bitcast_fusion
  51.0 0.2 fusion.31
  51.2 0.2 copy.51
  51.4 0.2 fusion.22
  51.6 0.2 fusion.12
  51.9 0.5 broadcast_in_dim.82
  52.4 38.5 %all_to_all.31 = bf16[64,4,2048]{2,1,0:T(4,128)(2,1)S(1)} all-to-all(bf16[64,4,2048]{2,1,0:T(4,128)(2,1)S(1)} %broadcast_in_dim.82), channel_id=1, replica_groups=mesh['grp'=8,'req'=64] {'req'}, dimensions={0} | all-to-all | bytes 2097152 | tf_op jit(solution)/shard_map/all_to_all | solution.py:76
  90.9 0.6 broadcast_in_dim.84
  91.6 5.9 %all-to-all-start.4 = ((bf16[64,1,64]{2,1,0:T(2,128)(2,1)}), bf16[64,1,64]{2,1,0:T(2,128)(2,1)S(1)}, u32[]{:S(2)}, u32[]{:S(2)}) async-start(bf16[64,1,64]{2,1,0:T(2,128)(2,1)} %broadcast_in_dim.84), calls=%async_computation.4 | async-start | bytes 65536 | tf_op jit(solution)/shard_map/all_to_all | solution.py:76
  97.5 1.1 reshape.92
  98.6 1.7 fusion.8
  100.3 6.6 %all-to-all-done.4 = bf16[64,1,64]{2,1,0:T(2,128)(2,1)S(1)} async-done(((bf16[64,1,64]{2,1,0:T(2,128)(2,1)}), bf16[64,1,64]{2,1,0:T(2,128)(2,1)S(1)}, u32[]{:S(2)}, u32[]{:S(2)}) %all-to-all-start.4) | async-done | bytes 8224 | tf_op jit(solution)/shard_map/all_to_all | solution.py:76
  106.9 1.5 broadcast_in_dim.83
  108.5 6.4 %all-to-all-start.3 = ((bf16[64,256,64]{1,2,0:T(8,128)(2,1)}), bf16[64,256,64]{1,2,0:T(8,128)(2,1)}, u32[]{:S(2)}, u32[]{:S(2)}) async-start(bf16[64,256,64]{1,2,0:T(8,128)(2,1)} %broadcast_in_dim.83), calls=%async_computation.3 | async-start | bytes 4194304 | tf_op jit(solution)/shard_map/all_to_all | solution.py:76
  114.9 1.6 copy.57
  116.5 0.1 convert_reduce_fusion.1
  116.7 46.1 %all-to-all-done.3 = bf16[64,256,64]{1,2,0:T(8,128)(2,1)} async-done(((bf16[64,256,64]{1,2,0:T(8,128)(2,1)}), bf16[64,256,64]{1,2,0:T(8,128)(2,1)}, u32[]{:S(2)}, u32[]{:S(2)}) %all-to-all-start.3) | async-done | bytes 2097184 | tf_op jit(solution)/shard_map/all_to_all | solution.py:76
  162.8 2.2 multiply_reduce_fusion
  165.0 1.9 fusion.1
  166.9 0.8 fusion.5
  167.7 2.0 convert_bitcast_fusion
  169.7 6.8 %all-to-all-start.5 = ((bf16[64,256,64]{1,2,0:T(8,128)(2,1)}), bf16[64,256,64]{1,2,0:T(8,128)(2,1)}, u32[]{:S(2)}, u32[]{:S(2)}) async-start(bf16[64,256,64]{1,2,0:T(8,128)(2,1)} %convert_bitcast_fusion), calls=%async_computation.5 | async-start | bytes 4194304 | tf_op jit(solution)/shard_map/all_to_all | solution.py:122
  176.6 0.1 reshape.93
  176.8 48.3 %all-to-all-done.5 = bf16[64,256,64]{1,2,0:T(8,128)(2,1)} async-done(((bf16[64,256,64]{1,2,0:T(8,128)(2,1)}), bf16[64,256,64]{1,2,0:T(8,128)(2,1)}, u32[]{:S(2)}, u32[]{:S(2)}) %all-to-all-start.5) | async-done | bytes 2097184 | tf_op jit(solution)/shard_map/all_to_all | solution.py:122
  225.0 1.9 convert_reduce_fusion
  226.9 0.6 fusion.28
  (24 shorter events, 0.3 us)
Async XLA Ops:
  0.0 166.9 %copy-start = (bf16[2,4096,128]{2,1,0:T(8,128)(2,1)S(1)}, bf16[2,4096,128]{2,1,0:T(8,128)(2,1)}, u32[]{:S(2)}) copy-start(bf16[2,4096,128]{2,1,0:T(8,128)(2,1)} %param.18) | copy-start | bytes 6291460
  1.6 20.2 %all-to-all-start = ((bf16[8,4,2048]{2,1,0:T(4,128)(2,1)}), bf16[8,4,2048]{2,1,0:T(4,128)(2,1)S(1)}, u32[]{:S(2)}, u32[]{:S(2)}) async-start(bf16[8,4,2048]{2,1,0:T(4,128)(2,1)} %broadcast_in_dim.76), calls=%async_computation | async-start | bytes 262144 | tf_op jit(solution)/shard_map/all_to_all | solution.py:24
  24.6 7.3 %copy-start.3 = (bf16[1,1,4,2048]{3,2,1,0:T(4,128)(2,1)S(1)}, bf16[1,1,4,2048]{3,2,1,0:T(4,128)(2,1)}, u32[]{:S(2)}) copy-start(bf16[1,1,4,2048]{3,2,1,0:T(4,128)(2,1)} %param.10) | copy-start | bytes 49156
  24.6 7.3 %copy-start.6 = (bf16[1,1,2,4,512]{4,3,2,1,0:T(4,128)(2,1)S(1)}, bf16[1,1,2,4,512]{4,3,2,1,0:T(4,128)(2,1)}, u32[]{:S(2)}) copy-start(bf16[1,1,2,4,512]{4,3,2,1,0:T(4,128)(2,1)} %param.11) | copy-start | bytes 24580
  28.4 21.3 %all-to-all-start.1 = ((f32[8,4,4,4,130]{4,3,2,1,0:T(4,128)}), f32[8,4,4,4,130]{4,3,2,1,0:T(4,128)S(1)}, u32[]{:S(2)}, u32[]{:S(2)}) async-start(f32[8,4,4,4,130]{4,3,2,1,0:T(4,128)} %maximum_bitcast_fusion), calls=%async_computation.1 | async-start | bytes 1048576 | tf_op jit(solution)/shard_map/all_to_all | solution.py:47
  51.0 40.0 %copy-start.4 = (bf16[64]{0:T(256)(128)(2,1)S(1)}, bf16[64]{0:T(256)(128)(2,1)}, u32[]{:S(2)}) copy-start(bf16[64]{0:T(256)(128)(2,1)} %param.17) | copy-start | bytes 388
  52.4 46.2 %copy-start.1 = (bf16[2048,64]{0,1:T(8,128)(2,1)S(1)}, bf16[2048,64]{0,1:T(8,128)(2,1)}, u32[]{:S(2)}) copy-start(bf16[2048,64]{0,1:T(8,128)(2,1)} %param.16) | copy-start | bytes 786436
  52.4 46.2 %copy-start.2 = (bf16[1,256,64]{1,2,0:T(8,128)(2,1)S(1)}, bf16[1,256,64]{1,2,0:T(8,128)(2,1)}, u32[]{:S(2)}) copy-start(bf16[1,256,64]{1,2,0:T(8,128)(2,1)} %param.15) | copy-start | bytes 98308
  91.6 15.3 %all-to-all-start.4 = ((bf16[64,1,64]{2,1,0:T(2,128)(2,1)}), bf16[64,1,64]{2,1,0:T(2,128)(2,1)S(1)}, u32[]{:S(2)}, u32[]{:S(2)}) async-start(bf16[64,1,64]{2,1,0:T(2,128)(2,1)} %broadcast_in_dim.84), calls=%async_computation.4 | async-start | bytes 65536 | tf_op jit(solution)/shard_map/all_to_all | solution.py:76
  108.5 54.3 %all-to-all-start.3 = ((bf16[64,256,64]{1,2,0:T(8,128)(2,1)}), bf16[64,256,64]{1,2,0:T(8,128)(2,1)}, u32[]{:S(2)}, u32[]{:S(2)}) async-start(bf16[64,256,64]{1,2,0:T(8,128)(2,1)} %broadcast_in_dim.83), calls=%async_computation.3 | async-start | bytes 4194304 | tf_op jit(solution)/shard_map/all_to_all | solution.py:76
  169.7 6.8 %copy-start.5 = (s32[1,64]{1,0:T(1,128)S(1)}, s32[1,64]{1,0:T(1,128)}, u32[]{:S(2)}) copy-start(s32[1,64]{1,0:T(1,128)} %param.14) | copy-start | bytes 772
  169.7 55.3 %all-to-all-start.5 = ((bf16[64,256,64]{1,2,0:T(8,128)(2,1)}), bf16[64,256,64]{1,2,0:T(8,128)(2,1)}, u32[]{:S(2)}, u32[]{:S(2)}) async-start(bf16[64,256,64]{1,2,0:T(8,128)(2,1)} %convert_bitcast_fusion), calls=%async_computation.5 | async-start | bytes 4194304 | tf_op jit(solution)/shard_map/all_to_all | solution.py:122

commit v4 on v3

--- a/solution.py
+++ b/solution.py
@@ -90,10 +90,13 @@
 ):
     slot_count = queries.shape[2]
     req_count = lax.psum(1, "req")
-    full_gain = gather_rows(norm_gain, req_count).reshape(-1)
     attention = attend(queries[0, 0], suffix_kv[0, 0], prefix_pool[0, 0], page_table[0])
+    gain_cols = norm_gain.shape[0] // slot_count
+    gain_block = jnp.pad(norm_gain.reshape(slot_count, gain_cols), ((0, 0), (0, HD - gain_cols)))
+    gathered_rows = gather_rows(jnp.concatenate([attention, gain_block], axis=1), req_count)
+    full_gain = gathered_rows[:, :, QH * HD : QH * HD + gain_cols].reshape(-1)
     projected = jnp.dot(
-        gather_rows(attention, req_count).reshape(-1, attention.shape[-1]),
+        gathered_rows[:, :, : QH * HD].reshape(-1, QH * HD),
         out_weight,
         preferred_element_type=jnp.float32,
     )

time: 228 us -> 220 us (0.965)
  starting transfers between devices: 32.9 us -> 26.4 us
  waiting for transfers between devices: 125 us -> 121 us
    all_to_all x2 -> x1, starting transfers between devices: 12.3 us -> 6.13 us  [gather_rows(): return lax.all_to_all(spread, 'req', 0, 0, tiled=False)]
    all_to_all x2 -> x1, waiting for transfers between devices: 52.8 us -> 47.2 us  [gather_rows(): return lax.all_to_all(spread, 'req', 0, 0, tiled=False)]
  transfers between devices with their start and end apart: 5 -> 4, of which waited for: 5 -> 4; matrix products, arithmetic and copies ran while one was open for 4% -> 3% of each run, Pallas kernels for 0% -> 0%
where the time goes in v4:
time: 220 us; the launch traced here: 219 us
  waiting for transfers between devices  121 us (55%)
  blocking collectives  39.8 us (18%)
  starting transfers between devices  26.4 us (12%)
  local copies, waits for them, and re-layouts  15.6 us (7%)
  other arithmetic  9.71 us (4%)
  matrix products  6.68 us (3%)
    all_to_all x1, waiting for transfers between devices, body(): lax.all_to_all(blocks.astype(jnp.bfloat16), 'req', 0, 0, tiled=False)  49.5 us
    all_to_all x1, waiting for transfers between devices, gather_rows(): return lax.all_to_all(spread, 'req', 0, 0, tiled=False)  47.2 us
    all_to_all x1, blocking collectives, gather_rows(): return lax.all_to_all(spread, 'req', 0, 0, tiled=False)  39.8 us
    all_to_all x1, waiting for transfers between devices, attend(): parts = lax.all_to_all(packed, 'grp', 0, 0, tiled=False)  17.4 us
    all_to_all x1, starting transfers between devices, attend(): all_queries = lax.all_to_all(spread, 'grp', 0, 0, tiled=False)  10.3 us
    all_to_all x1, waiting for transfers between devices, attend(): all_queries = lax.all_to_all(spread, 'grp', 0, 0, tiled=False)  6.88 us
    all_to_all x1, starting transfers between devices, body(): lax.all_to_all(blocks.astype(jnp.bfloat16), 'req', 0, 0, tiled=False)  6.47 us
    all_to_all x1, starting transfers between devices, gather_rows(): return lax.all_to_all(spread, 'req', 0, 0, tiled=False)  6.13 us
  transfers between devices with their start and end apart: 4, of which 4 were waited for; matrix products, arithmetic and copies ran while one was open for 3% of the time, Pallas kernels for 0%

profile of v4, /device:TPU:8, one launch (start us, length us, event | category | flops | bytes accessed | tf_op | source)
XLA Modules:
  0.0 219.5 jit_solution(5212827675401507134)
XLA Ops:
  0.0 1.6 broadcast_in_dim.70
  1.6 10.3 %all-to-all-start = ((bf16[8,4,2048]{2,1,0:T(4,128)(2,1)}), bf16[8,4,2048]{2,1,0:T(4,128)(2,1)S(1)}, u32[]{:S(2)}, u32[]{:S(2)}) async-start(bf16[8,4,2048]{2,1,0:T(4,128)(2,1)} %broadcast_in_dim.70), calls=%async_computation | async-start | bytes 262144 | tf_op jit(solution)/shard_map/all_to_all | solution.py:24
  11.9 1.2 fusion.47
  13.0 0.8 compare_reduce_fusion
  13.9 0.1 reshape_squeeze.15
  14.0 0.8 reshape_squeeze.16
  14.9 6.9 %all-to-all-done = bf16[8,4,2048]{2,1,0:T(4,128)(2,1)S(1)} async-done(((bf16[8,4,2048]{2,1,0:T(4,128)(2,1)}), bf16[8,4,2048]{2,1,0:T(4,128)(2,1)S(1)}, u32[]{:S(2)}, u32[]{:S(2)}) %all-to-all-start) | async-done | bytes 131104 | tf_op jit(solution)/shard_map/all_to_all | solution.py:24
  21.8 0.1 reshape_reshape.3
  21.9 0.4 fusion.49
  22.3 0.1 concatenate.14
  22.4 0.3 fusion.13
  22.7 0.1 concatenate.15
  22.8 0.9 copy.48
  23.7 0.9 copy.47
  24.6 1.3 fusion.15
  25.9 1.0 maximum_bitcast_fusion
  26.9 3.5 %all-to-all-start.1 = ((f32[8,4,4,4,130]{4,3,2,1,0:T(4,128)}), f32[8,4,4,4,130]{4,3,2,1,0:T(4,128)S(1)}, u32[]{:S(2)}, u32[]{:S(2)}) async-start(f32[8,4,4,4,130]{4,3,2,1,0:T(4,128)} %maximum_bitcast_fusion), calls=%async_computation.1 | async-start | bytes 1048576 | tf_op jit(solution)/shard_map/all_to_all | solution.py:47
  30.4 0.1 reshape.84
  30.5 0.3 fusion.50
  30.8 17.4 %all-to-all-done.1 = f32[8,4,4,4,130]{4,3,2,1,0:T(4,128)S(1)} async-done(((f32[8,4,4,4,130]{4,3,2,1,0:T(4,128)}), f32[8,4,4,4,130]{4,3,2,1,0:T(4,128)S(1)}, u32[]{:S(2)}, u32[]{:S(2)}) %all-to-all-start.1) | async-done | bytes 266272 | tf_op jit(solution)/shard_map/all_to_all | solution.py:47
  48.2 0.3 fusion.48
  48.5 0.5 copy.70
  49.0 0.1 exponential_bitcast_fusion
  49.1 0.2 copy.51
  49.2 0.5 copy.55
  49.7 0.2 fusion.32
  50.0 0.2 fusion.22
  50.2 0.2 fusion.12
  50.4 0.3 broadcast_in_dim.76
  50.7 39.8 %all_to_all.25 = bf16[64,4,2176]{2,1,0:T(4,128)(2,1)S(1)} all-to-all(bf16[64,4,2176]{2,1,0:T(4,128)(2,1)S(1)} %broadcast_in_dim.76), channel_id=1, replica_groups=mesh['grp'=8,'req'=64] {'req'}, dimensions={0} | all-to-all | bytes 2228224 | tf_op jit(solution)/shard_map/all_to_all | solution.py:76
  90.5 1.6 slice.51
  92.1 2.2 %reshape.85 = bf16[256,2048]{1,0:T(8,128)(2,1)} reshape(bf16[64,4,2048]{2,1,0:T(4,128)(2,1)} %slice.51) | data formatting | bytes 2097152 | tf_op jit(solution)/shard_map/reshape | solution.py:99
  94.3 1.7 fusion.8
  96.0 1.6 broadcast_in_dim.77
  97.5 6.1 %all-to-all-start.3 = ((bf16[64,256,64]{1,2,0:T(8,128)(2,1)}), bf16[64,256,64]{1,2,0:T(8,128)(2,1)}, u32[]{:S(2)}, u32[]{:S(2)}) async-start(bf16[64,256,64]{1,2,0:T(8,128)(2,1)} %broadcast_in_dim.77), calls=%async_computation.3 | async-start | bytes 4194304 | tf_op jit(solution)/shard_map/all_to_all | solution.py:76
  103.7 2.3 %copy.57 = bf16[128,4096]{0,1:T(8,128)(2,1)} copy(bf16[128,4096]{1,0:T(8,128)(2,1)} %param.19) | data formatting | bytes 2097152 | tf_op args[9]
  106.0 0.1 reshape.89
  106.1 47.2 %all-to-all-done.3 = bf16[64,256,64]{1,2,0:T(8,128)(2,1)} async-done(((bf16[64,256,64]{1,2,0:T(8,128)(2,1)}), bf16[64,256,64]{1,2,0:T(8,128)(2,1)}, u32[]{:S(2)}, u32[]{:S(2)}) %all-to-all-start.3) | async-done | bytes 2097184 | tf_op jit(solution)/shard_map/all_to_all | solution.py:76
  153.4 2.2 multiply_reduce_fusion
  155.5 1.9 fusion.1
  157.5 0.8 fusion.5
  158.3 0.5 copy-done.1
  158.7 2.0 convert_bitcast_fusion
  160.7 6.5 %all-to-all-start.4 = ((bf16[64,256,64]{1,2,0:T(8,128)(2,1)}), bf16[64,256,64]{1,2,0:T(8,128)(2,1)}, u32[]{:S(2)}, u32[]{:S(2)}) async-start(bf16[64,256,64]{1,2,0:T(8,128)(2,1)} %convert_bitcast_fusion), calls=%async_computation.4 | async-start | bytes 4194304 | tf_op jit(solution)/shard_map/all_to_all | solution.py:125
  167.3 0.1 reshape.86
  167.4 49.5 %all-to-all-done.4 = bf16[64,256,64]{1,2,0:T(8,128)(2,1)} async-done(((bf16[64,256,64]{1,2,0:T(8,128)(2,1)}), bf16[64,256,64]{1,2,0:T(8,128)(2,1)}, u32[]{:S(2)}, u32[]{:S(2)}) %all-to-all-start.4) | async-done | bytes 2097184 | tf_op jit(solution)/shard_map/all_to_all | solution.py:125
  217.0 1.9 convert_reduce_fusion
  218.9 0.6 fusion.29
  (24 shorter events, 0.3 us)
Async XLA Ops:
  0.0 157.5 %copy-start = (bf16[2,4096,128]{2,1,0:T(8,128)(2,1)S(1)}, bf16[2,4096,128]{2,1,0:T(8,128)(2,1)}, u32[]{:S(2)}) copy-start(bf16[2,4096,128]{2,1,0:T(8,128)(2,1)} %param.18) | copy-start | bytes 6291460
  1.6 20.2 %all-to-all-start = ((bf16[8,4,2048]{2,1,0:T(4,128)(2,1)}), bf16[8,4,2048]{2,1,0:T(4,128)(2,1)S(1)}, u32[]{:S(2)}, u32[]{:S(2)}) async-start(bf16[8,4,2048]{2,1,0:T(4,128)(2,1)} %broadcast_in_dim.70), calls=%async_computation | async-start | bytes 262144 | tf_op jit(solution)/shard_map/all_to_all | solution.py:24
  23.6 6.8 %copy-start.6 = (bf16[64]{0:T(256)(128)(2,1)S(1)}, bf16[64]{0:T(256)(128)(2,1)}, u32[]{:S(2)}) copy-start(bf16[64]{0:T(256)(128)(2,1)} %param.17) | copy-start | bytes 388
  23.6 6.9 %copy-start.3 = (bf16[1,1,4,2048]{3,2,1,0:T(4,128)(2,1)S(1)}, bf16[1,1,4,2048]{3,2,1,0:T(4,128)(2,1)}, u32[]{:S(2)}) copy-start(bf16[1,1,4,2048]{3,2,1,0:T(4,128)(2,1)} %param.10) | copy-start | bytes 49156
  23.7 6.9 %copy-start.5 = (bf16[1,1,2,4,512]{4,3,2,1,0:T(4,128)(2,1)S(1)}, bf16[1,1,2,4,512]{4,3,2,1,0:T(4,128)(2,1)}, u32[]{:S(2)}) copy-start(bf16[1,1,2,4,512]{4,3,2,1,0:T(4,128)(2,1)} %param.11) | copy-start | bytes 24580
  26.9 21.3 %all-to-all-start.1 = ((f32[8,4,4,4,130]{4,3,2,1,0:T(4,128)}), f32[8,4,4,4,130]{4,3,2,1,0:T(4,128)S(1)}, u32[]{:S(2)}, u32[]{:S(2)}) async-start(f32[8,4,4,4,130]{4,3,2,1,0:T(4,128)} %maximum_bitcast_fusion), calls=%async_computation.1 | async-start | bytes 1048576 | tf_op jit(solution)/shard_map/all_to_all | solution.py:47
  90.5 3.8 %copy-start.2 = (bf16[1,256,64]{1,2,0:T(8,128)(2,1)S(1)}, bf16[1,256,64]{1,2,0:T(8,128)(2,1)}, u32[]{:S(2)}) copy-start(bf16[1,256,64]{1,2,0:T(8,128)(2,1)} %param.15) | copy-start | bytes 98308
  97.5 55.8 %all-to-all-start.3 = ((bf16[64,256,64]{1,2,0:T(8,128)(2,1)}), bf16[64,256,64]{1,2,0:T(8,128)(2,1)}, u32[]{:S(2)}, u32[]{:S(2)}) async-start(bf16[64,256,64]{1,2,0:T(8,128)(2,1)} %broadcast_in_dim.77), calls=%async_computation.3 | async-start | bytes 4194304 | tf_op jit(solution)/shard_map/all_to_all | solution.py:76
  157.5 1.2 copy-start.1
  160.7 6.5 %copy-start.4 = (s32[1,64]{1,0:T(1,128)S(1)}, s32[1,64]{1,0:T(1,128)}, u32[]{:S(2)}) copy-start(s32[1,64]{1,0:T(1,128)} %param.14) | copy-start | bytes 772
  160.7 56.2 %all-to-all-start.4 = ((bf16[64,256,64]{1,2,0:T(8,128)(2,1)}), bf16[64,256,64]{1,2,0:T(8,128)(2,1)}, u32[]{:S(2)}, u32[]{:S(2)}) async-start(bf16[64,256,64]{1,2,0:T(8,128)(2,1)} %convert_bitcast_fusion), calls=%async_computation.4 | async-start | bytes 4194304 | tf_op jit(solution)/shard_map/all_to_all | solution.py:125

commit v5 on v4

--- a/solution.py
+++ b/solution.py
@@ -95,16 +95,27 @@
     gain_block = jnp.pad(norm_gain.reshape(slot_count, gain_cols), ((0, 0), (0, HD - gain_cols)))
     gathered_rows = gather_rows(jnp.concatenate([attention, gain_block], axis=1), req_count)
     full_gain = gathered_rows[:, :, QH * HD : QH * HD + gain_cols].reshape(-1)
+    token_count = residual.shape[1]
+    live_count = token_count // 2
+    lengths = suffix_len[0]
+    slot_index = jnp.arange(token_count, dtype=jnp.int32) % slot_count
+    slot_live = slot_index < jnp.repeat(lengths, slot_count)
+    live_rank = jnp.cumsum(slot_live.astype(jnp.int32)) - 1
+    live_rows = jnp.zeros((live_count,), jnp.int32).at[
+        jnp.where(slot_live, live_rank, live_count)
+    ].set(jnp.arange(token_count, dtype=jnp.int32), mode="drop")
+    all_rows = gathered_rows[:, :, : QH * HD].reshape(-1, QH * HD)
     projected = jnp.dot(
-        gathered_rows[:, :, : QH * HD].reshape(-1, QH * HD),
+        jnp.take(all_rows, live_rows, axis=0),
         out_weight,
         preferred_element_type=jnp.float32,
     )
-    stream = (residual[0].astype(jnp.float32) + projected).astype(jnp.bfloat16)
+    own_residual = jnp.take(residual[0], live_rows, axis=0)
+    stream = (own_residual.astype(jnp.float32) + projected).astype(jnp.bfloat16)
     wide_local = stream.astype(jnp.float32)
-    token_count, local_width = stream.shape
+    local_width = stream.shape[1]
     gathered = gather_rows(stream, req_count)
-    full_stream = jnp.transpose(gathered, (1, 0, 2)).reshape(token_count, -1)
+    full_stream = jnp.transpose(gathered, (1, 0, 2)).reshape(live_count, -1)
     wide = full_stream.astype(jnp.float32)
     row_sumsq = jnp.sum(wide * wide, axis=1)
     inverse_rms = lax.rsqrt(row_sumsq / D + 1e-05)
@@ -120,14 +131,12 @@
     hidden = (jax.nn.silu(gate_up_out[0]) * gate_up_out[1]).astype(jnp.bfloat16)
     partial_value = jnp.dot(hidden, down_weight, preferred_element_type=jnp.float32)
     blocks = jnp.transpose(
-        partial_value.reshape(token_count, req_count, local_width), (1, 0, 2)
+        partial_value.reshape(live_count, req_count, local_width), (1, 0, 2)
     )
     arrived = lax.all_to_all(blocks.astype(jnp.bfloat16), "req", 0, 0, tiled=False)
     summed = jnp.sum(arrived.astype(jnp.float32), axis=0)
-    lengths = suffix_len[0]
-    slot_index = jnp.arange(stream.shape[0], dtype=jnp.int32) % slot_count
-    slot_live = (slot_index < jnp.repeat(lengths, slot_count)).astype(jnp.float32)
-    result_rows = (wide_local + summed) * slot_live[:, None]
+    live_values = (wide_local + summed).astype(jnp.bfloat16)
+    result_rows = jnp.zeros((token_count, local_width), jnp.bfloat16).at[live_rows].set(live_values)
     return result_rows.astype(jnp.bfloat16)[None]
 
 

time: 220 us -> 172 us (0.78)
  waiting for transfers between devices: 121 us -> 72.7 us
  local copies, waits for them, and re-layouts: 15.6 us -> 23.5 us
  blocking collectives: 39.8 us -> 32.9 us
  starting transfers between devices: 26.4 us -> 30.9 us
  other arithmetic: 9.71 us -> 6.45 us
    all_to_all x1 -> x0, waiting for transfers between devices: 49.5 us -> none  [body(): lax.all_to_all(blocks.astype(jnp.bfloat16), 'req', 0, 0, tiled=False)]
    all_to_all x1 -> x2, starting transfers between devices: 6.13 us -> 17.1 us  [gather_rows(): return lax.all_to_all(spread, 'req', 0, 0, tiled=False)]
    all_to_all x1, blocking collectives: 39.8 us -> 32.9 us  [body(): lax.all_to_all(blocks.astype(jnp.bfloat16), 'req', 0, 0, tiled=False)]
    all_to_all x1 -> x0, starting transfers between devices: 6.47 us -> none  [body(): lax.all_to_all(blocks.astype(jnp.bfloat16), 'req', 0, 0, tiled=False)]
    gather x0 -> x3, local copies, waits for them, and re-layouts: none -> 2.54 us  [the longest x1 1.74 us: body(): jnp.take(all_rows, live_rows, axis=0)]
    scatter x0 -> x2, local copies, waits for them, and re-layouts: none -> 2.31 us  [the longest x1 1.4 us: body(): live_rows = jnp.zeros((live_count,), jnp.int32).at[jnp.where(slot_live, l...]
    unnamed x16 -> x20, local copies, waits for them, and re-layouts: 3.24 us -> 5.08 us
    all_to_all x1 -> x2, waiting for transfers between devices: 47.2 us -> 48.5 us  [gather_rows(): return lax.all_to_all(spread, 'req', 0, 0, tiled=False)]
  transfers between devices with their start and end apart: 4 -> 4, of which waited for: 4 -> 4; matrix products, arithmetic and copies ran while one was open for 3% -> 7% of each run, Pallas kernels for 0% -> 0%
where the time goes in v5:
time: 172 us; the launch traced here: 171 us
  waiting for transfers between devices  72.7 us (42%)
  blocking collectives  32.9 us (19%)
  starting transfers between devices  30.9 us (18%)
  local copies, waits for them, and re-layouts  23.5 us (14%)
  other arithmetic  6.45 us (4%)
  matrix products  4.64 us (3%)
    all_to_all x2, waiting for transfers between devices, gather_rows(): return lax.all_to_all(spread, 'req', 0, 0, tiled=False)  48.5 us
    all_to_all x1, blocking collectives, body(): lax.all_to_all(blocks.astype(jnp.bfloat16), 'req', 0, 0, tiled=False)  32.9 us
    all_to_all x1, waiting for transfers between devices, attend(): parts = lax.all_to_all(packed, 'grp', 0, 0, tiled=False)  17.4 us
    all_to_all x2, starting transfers between devices, gather_rows(): return lax.all_to_all(spread, 'req', 0, 0, tiled=False)  17.1 us
    all_to_all x1, starting transfers between devices, attend(): all_queries = lax.all_to_all(spread, 'grp', 0, 0, tiled=False)  10.3 us
    all_to_all x1, waiting for transfers between devices, attend(): all_queries = lax.all_to_all(spread, 'grp', 0, 0, tiled=False)  6.88 us
    unnamed x20, local copies, waits for them, and re-layouts  5.08 us
    all_to_all x1, starting transfers between devices, attend(): parts = lax.all_to_all(packed, 'grp', 0, 0, tiled=False)  3.49 us
  transfers between devices with their start and end apart: 4, of which 4 were waited for; matrix products, arithmetic and copies ran while one was open for 7% of the time, Pallas kernels for 0%

profile of v5, /device:TPU:8, one launch (start us, length us, event | category | flops | bytes accessed | tf_op | source)
XLA Modules:
  0.0 171.5 jit_solution(2752829357033195469)
XLA Ops:
  0.0 1.6 broadcast_in_dim.116
  1.6 10.3 %all-to-all-start = ((bf16[8,4,2048]{2,1,0:T(4,128)(2,1)}), bf16[8,4,2048]{2,1,0:T(4,128)(2,1)S(1)}, u32[]{:S(2)}, u32[]{:S(2)}) async-start(bf16[8,4,2048]{2,1,0:T(4,128)(2,1)} %broadcast_in_dim.116), calls=%async_computation | async-start | bytes 262144 | tf_op jit(solution)/shard_map/all_to_all | solution.py:24
  11.9 1.2 fusion.52
  13.0 0.8 compare_reduce_fusion
  14.0 0.8 reshape_squeeze.16
  14.9 6.9 %all-to-all-done = bf16[8,4,2048]{2,1,0:T(4,128)(2,1)S(1)} async-done(((bf16[8,4,2048]{2,1,0:T(4,128)(2,1)}), bf16[8,4,2048]{2,1,0:T(4,128)(2,1)S(1)}, u32[]{:S(2)}, u32[]{:S(2)}) %all-to-all-start) | async-done | bytes 131104 | tf_op jit(solution)/shard_map/all_to_all | solution.py:24
  21.9 0.4 fusion.54
  22.4 0.3 fusion.10
  22.7 1.3 fusion.14
  24.1 0.9 copy.60
  25.0 0.9 copy.59
  25.9 1.0 maximum_bitcast_fusion
  26.9 3.5 %all-to-all-start.1 = ((f32[8,4,4,4,130]{4,3,2,1,0:T(4,128)}), f32[8,4,4,4,130]{4,3,2,1,0:T(4,128)S(1)}, u32[]{:S(2)}, u32[]{:S(2)}) async-start(f32[8,4,4,4,130]{4,3,2,1,0:T(4,128)} %maximum_bitcast_fusion), calls=%async_computation.1 | async-start | bytes 1048576 | tf_op jit(solution)/shard_map/all_to_all | solution.py:47
  30.5 0.3 fusion.55
  30.8 17.4 %all-to-all-done.1 = f32[8,4,4,4,130]{4,3,2,1,0:T(4,128)S(1)} async-done(((f32[8,4,4,4,130]{4,3,2,1,0:T(4,128)}), f32[8,4,4,4,130]{4,3,2,1,0:T(4,128)S(1)}, u32[]{:S(2)}, u32[]{:S(2)}) %all-to-all-start.1) | async-done | bytes 266272 | tf_op jit(solution)/shard_map/all_to_all | solution.py:47
  48.2 0.3 fusion.53
  48.5 0.5 copy.84
  49.0 0.5 copy.67
  49.6 0.2 fusion.30
  49.8 0.2 copy.63
  50.0 0.2 fusion.21
  50.2 0.2 fusion.7
  50.5 1.3 broadcast_in_dim.122
  51.7 11.1 %all-to-all-start.2 = ((bf16[64,4,2176]{2,1,0:T(4,128)(2,1)}), bf16[64,4,2176]{2,1,0:T(4,128)(2,1)S(1)}, u32[]{:S(2)}, u32[]{:S(2)}) async-start(bf16[64,4,2176]{2,1,0:T(4,128)(2,1)} %broadcast_in_dim.122), calls=%async_computation.2 | async-start | bytes 2228224 | tf_op jit(solution)/shard_map/all_to_all | solution.py:76
  62.9 0.5 broadcast.138
  63.4 0.7 reduce.8
  64.4 0.3 reduce-window.9
  65.3 1.4 scatter_custom_fusion
  66.7 0.7 gather_fusion
  67.6 24.2 %all-to-all-done.2 = bf16[64,4,2176]{2,1,0:T(4,128)(2,1)S(1)} async-done(((bf16[64,4,2176]{2,1,0:T(4,128)(2,1)}), bf16[64,4,2176]{2,1,0:T(4,128)(2,1)S(1)}, u32[]{:S(2)}, u32[]{:S(2)}) %all-to-all-start.2) | async-done | bytes 1114144 | tf_op jit(solution)/shard_map/all_to_all | solution.py:76
  91.7 1.0 copy-done.1
  92.7 1.6 slice.64
  94.3 1.3 reshape.162
  95.7 1.7 %gather_fusion.1 = bf16[128,2048]{1,0:T(8,128)(2,1)} fusion(bf16[256,2048]{1,0:T(8,128)(2,1)S(1)} %reshape.162, s32[1024]{0:T(1024)S(1)} %pad_clamp_fusion), kind=kCustom, calls=%fused_computation.1 | custom fusion | bytes 1049088 | tf_op jit(solution)/shard_map/jit(_take)/gather | solution.py:109
  97.4 1.5 fusion.8
  98.9 1.3 broadcast_in_dim.124
  100.1 5.9 %all-to-all-start.3 = ((bf16[64,128,64]{1,2,0:T(8,128)(2,1)}), bf16[64,128,64]{1,2,0:T(8,128)(2,1)S(1)}, u32[]{:S(2)}, u32[]{:S(2)}) async-start(bf16[64,128,64]{1,2,0:T(8,128)(2,1)} %broadcast_in_dim.124), calls=%async_computation.3 | async-start | bytes 2097152 | tf_op jit(solution)/shard_map/all_to_all | solution.py:76
  106.1 2.3 %copy.69 = bf16[128,4096]{0,1:T(8,128)(2,1)} copy(bf16[128,4096]{1,0:T(8,128)(2,1)} %param.19) | data formatting | bytes 2097152 | tf_op args[9]
  108.3 0.9 slice_convert_fusion
  109.3 24.3 %all-to-all-done.3 = bf16[64,128,64]{1,2,0:T(8,128)(2,1)S(1)} async-done(((bf16[64,128,64]{1,2,0:T(8,128)(2,1)}), bf16[64,128,64]{1,2,0:T(8,128)(2,1)S(1)}, u32[]{:S(2)}, u32[]{:S(2)}) %all-to-all-start.3) | async-done | bytes 1048608 | tf_op jit(solution)/shard_map/all_to_all | solution.py:76
  133.6 0.6 multiply_reduce_fusion
  134.2 0.7 fusion.1
  134.9 0.5 convolution_bitcast_fusion
  135.4 0.7 copy-done.2
  136.1 0.4 fusion.2
  136.6 32.9 %all_to_all.25 = bf16[64,128,64]{1,2,0:T(8,128)(2,1)S(1)} all-to-all(bf16[64,128,64]{1,2,0:T(8,128)(2,1)S(1)} %fusion.2), channel_id=1, replica_groups=mesh['grp'=8,'req'=64] {'req'}, dimensions={0} | all-to-all | bytes 2097152 | tf_op jit(solution)/shard_map/all_to_all | solution.py:136
  169.8 0.9 scatter_custom_fusion.1
  170.8 0.7 copy.71
  (49 shorter events, 2.1 us)
Async XLA Ops:
  0.0 134.9 %copy-start = (bf16[2,4096,128]{2,1,0:T(8,128)(2,1)S(1)}, bf16[2,4096,128]{2,1,0:T(8,128)(2,1)}, u32[]{:S(2)}) copy-start(bf16[2,4096,128]{2,1,0:T(8,128)(2,1)} %param.18) | copy-start | bytes 6291460
  1.6 20.2 %all-to-all-start = ((bf16[8,4,2048]{2,1,0:T(4,128)(2,1)}), bf16[8,4,2048]{2,1,0:T(4,128)(2,1)S(1)}, u32[]{:S(2)}, u32[]{:S(2)}) async-start(bf16[8,4,2048]{2,1,0:T(4,128)(2,1)} %broadcast_in_dim.116), calls=%async_computation | async-start | bytes 262144 | tf_op jit(solution)/shard_map/all_to_all | solution.py:24
  22.7 7.8 %copy-start.7 = (bf16[64]{0:T(256)(128)(2,1)S(1)}, bf16[64]{0:T(256)(128)(2,1)}, u32[]{:S(2)}) copy-start(bf16[64]{0:T(256)(128)(2,1)} %param.17) | copy-start | bytes 388
  22.7 7.9 %copy-start.4 = (bf16[1,1,4,2048]{3,2,1,0:T(4,128)(2,1)S(1)}, bf16[1,1,4,2048]{3,2,1,0:T(4,128)(2,1)}, u32[]{:S(2)}) copy-start(bf16[1,1,4,2048]{3,2,1,0:T(4,128)(2,1)} %param.10) | copy-start | bytes 49156
  22.7 7.9 %copy-start.6 = (bf16[1,1,2,4,512]{4,3,2,1,0:T(4,128)(2,1)S(1)}, bf16[1,1,2,4,512]{4,3,2,1,0:T(4,128)(2,1)}, u32[]{:S(2)}) copy-start(bf16[1,1,2,4,512]{4,3,2,1,0:T(4,128)(2,1)} %param.11) | copy-start | bytes 24580
  26.9 21.3 %all-to-all-start.1 = ((f32[8,4,4,4,130]{4,3,2,1,0:T(4,128)}), f32[8,4,4,4,130]{4,3,2,1,0:T(4,128)S(1)}, u32[]{:S(2)}, u32[]{:S(2)}) async-start(f32[8,4,4,4,130]{4,3,2,1,0:T(4,128)} %maximum_bitcast_fusion), calls=%async_computation.1 | async-start | bytes 1048576 | tf_op jit(solution)/shard_map/all_to_all | solution.py:47
  50.0 13.4 %copy-start.5 = (s32[1,64]{1,0:T(1,128)S(1)}, s32[1,64]{1,0:T(1,128)}, u32[]{:S(2)}) copy-start(s32[1,64]{1,0:T(1,128)} %param.14) | copy-start | bytes 772
  50.0 15.0 %copy-start.3 = (bf16[1,256,64]{1,2,0:T(8,128)(2,1)S(1)}, bf16[1,256,64]{1,2,0:T(8,128)(2,1)}, u32[]{:S(2)}) copy-start(bf16[1,256,64]{1,2,0:T(8,128)(2,1)} %param.15) | copy-start | bytes 98308
  51.7 40.0 %all-to-all-start.2 = ((bf16[64,4,2176]{2,1,0:T(4,128)(2,1)}), bf16[64,4,2176]{2,1,0:T(4,128)(2,1)S(1)}, u32[]{:S(2)}, u32[]{:S(2)}) async-start(bf16[64,4,2176]{2,1,0:T(4,128)(2,1)} %broadcast_in_dim.122), calls=%async_computation.2 | async-start | bytes 2228224 | tf_op jit(solution)/shard_map/all_to_all | solution.py:76
  91.7 1.0 copy-start.1
  100.1 33.5 %all-to-all-start.3 = ((bf16[64,128,64]{1,2,0:T(8,128)(2,1)}), bf16[64,128,64]{1,2,0:T(8,128)(2,1)S(1)}, u32[]{:S(2)}, u32[]{:S(2)}) async-start(bf16[64,128,64]{1,2,0:T(8,128)(2,1)} %broadcast_in_dim.124), calls=%async_computation.3 | async-start | bytes 2097152 | tf_op jit(solution)/shard_map/all_to_all | solution.py:76
  134.9 1.2 copy-start.2

commit v6 on v5

--- a/solution.py
+++ b/solution.py
@@ -104,9 +104,9 @@
     live_rows = jnp.zeros((live_count,), jnp.int32).at[
         jnp.where(slot_live, live_rank, live_count)
     ].set(jnp.arange(token_count, dtype=jnp.int32), mode="drop")
-    all_rows = gathered_rows[:, :, : QH * HD].reshape(-1, QH * HD)
+    live_heads = gathered_rows[live_rows // slot_count, live_rows % slot_count, : QH * HD]
     projected = jnp.dot(
-        jnp.take(all_rows, live_rows, axis=0),
+        live_heads,
         out_weight,
         preferred_element_type=jnp.float32,
     )

time: 172 us -> 698 us (4.06); the launches traced: 171 us -> 685 us
  local copies, waits for them, and re-layouts: 23.5 us -> 540 us
    gather x1 -> x512, local copies, waits for them, and re-layouts: 1.74 us -> 517 us  [body(): jnp.take(all_rows, live_rows, axis=0)]
  transfers between devices with their start and end apart: 4 -> 4, of which waited for: 4 -> 4; matrix products, arithmetic and copies ran while one was open for 7% -> 2% of each run, Pallas kernels for 0% -> 0%
where the time goes in v6:
time: 698 us; the launch traced here: 685 us
  local copies, waits for them, and re-layouts  540 us (77%)
  waiting for transfers between devices  68.1 us (10%)
  blocking collectives  33 us (5%)
  starting transfers between devices  30.9 us (4%)
  other arithmetic  7.9 us (1%)
    gather x512, local copies, waits for them, and re-layouts  517 us
    all_to_all x2, waiting for transfers between devices, gather_rows(): return lax.all_to_all(spread, 'req', 0, 0, tiled=False)  43.8 us
    all_to_all x1, blocking collectives, body(): lax.all_to_all(blocks.astype(jnp.bfloat16), 'req', 0, 0, tiled=False)  33 us
    all_to_all x1, waiting for transfers between devices, attend(): parts = lax.all_to_all(packed, 'grp', 0, 0, tiled=False)  17.4 us
    all_to_all x2, starting transfers between devices, gather_rows(): return lax.all_to_all(spread, 'req', 0, 0, tiled=False)  17.1 us
  transfers between devices with their start and end apart: 4, of which 4 were waited for; matrix products, arithmetic and copies ran while one was open for 2% of the time, Pallas kernels for 0%

profile of v6, /device:TPU:8, one launch (start us, length us, event | category | flops | bytes accessed | tf_op | source)
XLA Modules:
  0.0 685.1 jit_solution(2396904944665690895)
XLA Ops:
  1.6 10.3 %all-to-all-start = ((bf16[8,4,2048]{2,1,0:T(4,128)(2,1)}), bf16[8,4,2048]{2,1,0:T(4,128)(2,1)S(1)}, u32[]{:S(2)}, u32[]{:S(2)}) async-start(bf16[8,4,2048]{2,1,0:T(4,128)(2,1)} %broadcast_in_dim.112), calls=%async_computation | async-start | bytes 262144 | tf_op jit(solution)/shard_map/all_to_all | solution.py:24
  14.9 6.9 %all-to-all-done = bf16[8,4,2048]{2,1,0:T(4,128)(2,1)S(1)} async-done(((bf16[8,4,2048]{2,1,0:T(4,128)(2,1)}), bf16[8,4,2048]{2,1,0:T(4,128)(2,1)S(1)}, u32[]{:S(2)}, u32[]{:S(2)}) %all-to-all-start) | async-done | bytes 131104 | tf_op jit(solution)/shard_map/all_to_all | solution.py:24
  28.4 3.5 all-to-all-start.1
  32.3 17.4 %all-to-all-done.1 = f32[8,4,4,4,130]{4,3,2,1,0:T(4,128)S(1)} async-done(((f32[8,4,4,4,130]{4,3,2,1,0:T(4,128)}), f32[8,4,4,4,130]{4,3,2,1,0:T(4,128)S(1)}, u32[]{:S(2)}, u32[]{:S(2)}) %all-to-all-start.1) | async-done | bytes 266272 | tf_op jit(solution)/shard_map/all_to_all | solution.py:47
  53.2 11.1 %all-to-all-start.2 = ((bf16[64,4,2176]{2,1,0:T(4,128)(2,1)}), bf16[64,4,2176]{2,1,0:T(4,128)(2,1)S(1)}, u32[]{:S(2)}, u32[]{:S(2)}) async-start(bf16[64,4,2176]{2,1,0:T(4,128)(2,1)} %broadcast_in_dim.118), calls=%async_computation.2 | async-start | bytes 2228224 | tf_op jit(solution)/shard_map/all_to_all | solution.py:76
  73.7 19.5 %all-to-all-done.2 = bf16[64,4,2176]{2,1,0:T(4,128)(2,1)S(1)} async-done(((bf16[64,4,2176]{2,1,0:T(4,128)(2,1)}), bf16[64,4,2176]{2,1,0:T(4,128)(2,1)S(1)}, u32[]{:S(2)}, u32[]{:S(2)}) %all-to-all-start.2) | async-done | bytes 1114144 | tf_op jit(solution)/shard_map/all_to_all | solution.py:76
  93.2 517.5 %while.1 = (s32[]{:T(128)}, bf16[64,4,2176]{2,1,0:T(4,128)(2,1)S(1)}, s32[128,3]{0,1:T(4,128)S(1)}, bf16[128,2048]{1,0:T(8,128)(2,1)}, s32[]{:T(128)}, /*index=5*/s32[]{:T(128)}) while((s32[]{:T(128)}, bf16[64,4,2176]{2,1,0:T(4,128)(2,1)S(1)}, s32[128,3]{0,1:T(4,128)S(1)}, bf16[128,2048]{1,0:T(8,128)(2,1)}, s32[]{:T(128)}, /*index=5*/s32[]{:T(128)}) %tuple.27), condition=%wide.while_cond, body=%wide.while_body.sunk | while | flops 2 | bytes 16521 | solution.py:107
  93.8 2.0 dynamic-slice_bitcast_fusion.2
  97.9 2.0 dynamic-slice_bitcast_fusion.2
  101.9 2.0 dynamic-slice_bitcast_fusion.2
  106.0 2.0 dynamic-slice_bitcast_fusion.2
  110.0 2.0 dynamic-slice_bitcast_fusion.2
  114.1 2.0 dynamic-slice_bitcast_fusion.2
  118.1 2.0 dynamic-slice_bitcast_fusion.2
  122.2 2.0 dynamic-slice_bitcast_fusion.2
  126.2 2.0 dynamic-slice_bitcast_fusion.2
  130.3 2.0 dynamic-slice_bitcast_fusion.2
  134.3 2.0 dynamic-slice_bitcast_fusion.2
  138.4 2.0 dynamic-slice_bitcast_fusion.2
  142.4 2.0 dynamic-slice_bitcast_fusion.2
  146.5 2.0 dynamic-slice_bitcast_fusion.2
  150.5 2.0 dynamic-slice_bitcast_fusion.2
  154.5 2.0 dynamic-slice_bitcast_fusion.2
  158.6 2.0 dynamic-slice_bitcast_fusion.2
  162.6 2.0 dynamic-slice_bitcast_fusion.2
  166.7 2.0 dynamic-slice_bitcast_fusion.2
  174.8 2.0 dynamic-slice_bitcast_fusion.2
  203.1 2.0 dynamic-slice_bitcast_fusion.2
  215.2 2.0 dynamic-slice_bitcast_fusion.2
  227.3 2.0 dynamic-slice_bitcast_fusion.2
  255.6 2.0 dynamic-slice_bitcast_fusion.2
  267.8 2.0 dynamic-slice_bitcast_fusion.2
  328.4 2.0 dynamic-slice_bitcast_fusion.2
  344.6 2.0 dynamic-slice_bitcast_fusion.2
  352.7 2.0 dynamic-slice_bitcast_fusion.2
  405.2 2.0 dynamic-slice_bitcast_fusion.2
  441.6 2.0 dynamic-slice_bitcast_fusion.2
  482.1 2.0 dynamic-slice_bitcast_fusion.2
  494.2 2.0 dynamic-slice_bitcast_fusion.2
  506.3 2.0 dynamic-slice_bitcast_fusion.2
  538.6 2.0 dynamic-slice_bitcast_fusion.2
  542.7 2.0 dynamic-slice_bitcast_fusion.2
  554.8 2.0 dynamic-slice_bitcast_fusion.2
  566.9 2.0 dynamic-slice_bitcast_fusion.2
  613.6 5.9 all-to-all-start.3
  619.6 2.3 copy.69
  622.8 24.3 %all-to-all-done.3 = bf16[64,128,64]{1,2,0:T(8,128)(2,1)S(1)} async-done(((bf16[64,128,64]{1,2,0:T(8,128)(2,1)}), bf16[64,128,64]{1,2,0:T(8,128)(2,1)S(1)}, u32[]{:S(2)}, u32[]{:S(2)}) %all-to-all-start.3) | async-done | bytes 1048608 | tf_op jit(solution)/shard_map/all_to_all | solution.py:76
  650.1 33.0 %all_to_all.25 = bf16[64,128,64]{1,2,0:T(8,128)(2,1)S(1)} all-to-all(bf16[64,128,64]{1,2,0:T(8,128)(2,1)S(1)} %fusion.2), channel_id=1, replica_groups=mesh['grp'=8,'req'=64] {'req'}, dimensions={0} | all-to-all | bytes 2097152 | tf_op jit(solution)/shard_map/all_to_all | solution.py:136
  (564 shorter events, 477.0 us)
Async XLA Ops:
  0.0 648.4 %copy-start = (bf16[2,4096,128]{2,1,0:T(8,128)(2,1)S(1)}, bf16[2,4096,128]{2,1,0:T(8,128)(2,1)}, u32[]{:S(2)}) copy-start(bf16[2,4096,128]{2,1,0:T(8,128)(2,1)} %param.18) | copy-start | bytes 6291460
  1.6 20.2 %all-to-all-start = ((bf16[8,4,2048]{2,1,0:T(4,128)(2,1)}), bf16[8,4,2048]{2,1,0:T(4,128)(2,1)S(1)}, u32[]{:S(2)}, u32[]{:S(2)}) async-start(bf16[8,4,2048]{2,1,0:T(4,128)(2,1)} %broadcast_in_dim.112), calls=%async_computation | async-start | bytes 262144 | tf_op jit(solution)/shard_map/all_to_all | solution.py:24
  23.3 8.6 %copy-start.8 = (bf16[64]{0:T(256)(128)(2,1)S(1)}, bf16[64]{0:T(256)(128)(2,1)}, u32[]{:S(2)}) copy-start(bf16[64]{0:T(256)(128)(2,1)} %param.17) | copy-start | bytes 388
  24.6 7.4 %copy-start.4 = (bf16[1,1,4,2048]{3,2,1,0:T(4,128)(2,1)S(1)}, bf16[1,1,4,2048]{3,2,1,0:T(4,128)(2,1)}, u32[]{:S(2)}) copy-start(bf16[1,1,4,2048]{3,2,1,0:T(4,128)(2,1)} %param.10) | copy-start | bytes 49156
  24.6 7.3 %copy-start.7 = (bf16[1,1,2,4,512]{4,3,2,1,0:T(4,128)(2,1)S(1)}, bf16[1,1,2,4,512]{4,3,2,1,0:T(4,128)(2,1)}, u32[]{:S(2)}) copy-start(bf16[1,1,2,4,512]{4,3,2,1,0:T(4,128)(2,1)} %param.11) | copy-start | bytes 24580
  28.4 21.3 %all-to-all-start.1 = ((f32[8,4,4,4,130]{4,3,2,1,0:T(4,128)}), f32[8,4,4,4,130]{4,3,2,1,0:T(4,128)S(1)}, u32[]{:S(2)}, u32[]{:S(2)}) async-start(f32[8,4,4,4,130]{4,3,2,1,0:T(4,128)} %maximum_bitcast_fusion), calls=%async_computation.1 | async-start | bytes 1048576 | tf_op jit(solution)/shard_map/all_to_all | solution.py:47
  51.4 13.4 %copy-start.6 = (s32[1,64]{1,0:T(1,128)S(1)}, s32[1,64]{1,0:T(1,128)}, u32[]{:S(2)}) copy-start(s32[1,64]{1,0:T(1,128)} %param.14) | copy-start | bytes 772
  51.9 558.8 %copy-start.3 = (bf16[2048,64]{0,1:T(8,128)(2,1)S(1)}, bf16[2048,64]{0,1:T(8,128)(2,1)}, u32[]{:S(2)}) copy-start(bf16[2048,64]{0,1:T(8,128)(2,1)} %param.16) | copy-start | bytes 786436
  53.2 40.0 %all-to-all-start.2 = ((bf16[64,4,2176]{2,1,0:T(4,128)(2,1)}), bf16[64,4,2176]{2,1,0:T(4,128)(2,1)S(1)}, u32[]{:S(2)}, u32[]{:S(2)}) async-start(bf16[64,4,2176]{2,1,0:T(4,128)(2,1)} %broadcast_in_dim.118), calls=%async_computation.2 | async-start | bytes 2228224 | tf_op jit(solution)/shard_map/all_to_all | solution.py:76
  70.2 0.5 copy-start.5
  610.7 3.0 copy-start.2
  613.6 33.5 %all-to-all-start.3 = ((bf16[64,128,64]{1,2,0:T(8,128)(2,1)}), bf16[64,128,64]{1,2,0:T(8,128)(2,1)S(1)}, u32[]{:S(2)}, u32[]{:S(2)}) async-start(bf16[64,128,64]{1,2,0:T(8,128)(2,1)} %broadcast_in_dim.121), calls=%async_computation.3 | async-start | bytes 2097152 | tf_op jit(solution)/shard_map/all_to_all | solution.py:76
  648.4 1.2 copy-start.1

commit v7 on v6

--- a/solution.py
+++ b/solution.py
@@ -104,9 +104,9 @@
     live_rows = jnp.zeros((live_count,), jnp.int32).at[
         jnp.where(slot_live, live_rank, live_count)
     ].set(jnp.arange(token_count, dtype=jnp.int32), mode="drop")
-    live_heads = gathered_rows[live_rows // slot_count, live_rows % slot_count, : QH * HD]
+    all_rows = gathered_rows.reshape(token_count, -1)
     projected = jnp.dot(
-        live_heads,
+        jnp.take(all_rows, live_rows, axis=0)[:, : QH * HD],
         out_weight,
         preferred_element_type=jnp.float32,
     )

time: 698 us -> 171 us (0.24); the launches traced: 685 us -> 171 us
  local copies, waits for them, and re-layouts: 540 us -> 22.5 us
    gather x512 -> x1, local copies, waits for them, and re-layouts: 517 us -> 1.78 us  [body(): jnp.take(all_rows, live_rows, axis=0)[:, :QH * HD]]
  transfers between devices with their start and end apart: 4 -> 4, of which waited for: 4 -> 4; matrix products, arithmetic and copies ran while one was open for 2% -> 7% of each run, Pallas kernels for 0% -> 0%
where the time goes in v7:
time: 171 us
  waiting for transfers between devices  72.7 us (43%)
  blocking collectives  32.9 us (19%)
  starting transfers between devices  31 us (18%)
  local copies, waits for them, and re-layouts  22.5 us (13%)
  other arithmetic  6.45 us (4%)
  matrix products  4.64 us (3%)
    all_to_all x2, waiting for transfers between devices, gather_rows(): return lax.all_to_all(spread, 'req', 0, 0, tiled=False)  48.4 us
    all_to_all x1, blocking collectives, body(): lax.all_to_all(blocks.astype(jnp.bfloat16), 'req', 0, 0, tiled=False)  32.9 us
    all_to_all x1, waiting for transfers between devices, attend(): parts = lax.all_to_all(packed, 'grp', 0, 0, tiled=False)  17.4 us
    all_to_all x2, starting transfers between devices, gather_rows(): return lax.all_to_all(spread, 'req', 0, 0, tiled=False)  17.2 us
    all_to_all x1, starting transfers between devices, attend(): all_queries = lax.all_to_all(spread, 'grp', 0, 0, tiled=False)  10.3 us
    all_to_all x1, waiting for transfers between devices, attend(): all_queries = lax.all_to_all(spread, 'grp', 0, 0, tiled=False)  6.88 us
    unnamed x18, local copies, waits for them, and re-layouts  4.09 us
    all_to_all x1, starting transfers between devices, attend(): parts = lax.all_to_all(packed, 'grp', 0, 0, tiled=False)  3.49 us
  transfers between devices with their start and end apart: 4, of which 4 were waited for; matrix products, arithmetic and copies ran while one was open for 7% of the time, Pallas kernels for 0%

profile of v7, /device:TPU:8, one launch (start us, length us, event | category | flops | bytes accessed | tf_op | source)
XLA Modules:
  0.0 170.5 jit_solution(7769303872990367017)
XLA Ops:
  0.0 1.6 broadcast_in_dim.116
  1.6 10.3 %all-to-all-start = ((bf16[8,4,2048]{2,1,0:T(4,128)(2,1)}), bf16[8,4,2048]{2,1,0:T(4,128)(2,1)S(1)}, u32[]{:S(2)}, u32[]{:S(2)}) async-start(bf16[8,4,2048]{2,1,0:T(4,128)(2,1)} %broadcast_in_dim.116), calls=%async_computation | async-start | bytes 262144 | tf_op jit(solution)/shard_map/all_to_all | solution.py:24
  11.9 1.2 fusion.51
  13.0 0.8 compare_reduce_fusion
  14.0 0.8 reshape_squeeze.16
  14.9 6.9 %all-to-all-done = bf16[8,4,2048]{2,1,0:T(4,128)(2,1)S(1)} async-done(((bf16[8,4,2048]{2,1,0:T(4,128)(2,1)}), bf16[8,4,2048]{2,1,0:T(4,128)(2,1)S(1)}, u32[]{:S(2)}, u32[]{:S(2)}) %all-to-all-start) | async-done | bytes 131104 | tf_op jit(solution)/shard_map/all_to_all | solution.py:24
  21.9 0.4 fusion.53
  22.3 0.7 concatenate.14
  23.0 0.3 fusion.10
  23.3 1.3 fusion.13
  24.7 0.9 copy.60
  25.6 1.7 %copy.59 = f32[4,4,8,4,1]{4,3,1,0,2:T(4,128)S(1)} copy(f32[4,4,8,4,1]{3,2,1,0,4:T(8,128)} %concatenate.14) | data formatting | bytes 4096 | tf_op jit(solution)/shard_map/concatenate | solution.py:44
  27.3 1.0 maximum_bitcast_fusion
  28.4 3.5 %all-to-all-start.1 = ((f32[8,4,4,4,130]{4,3,2,1,0:T(4,128)}), f32[8,4,4,4,130]{4,3,2,1,0:T(4,128)S(1)}, u32[]{:S(2)}, u32[]{:S(2)}) async-start(f32[8,4,4,4,130]{4,3,2,1,0:T(4,128)} %maximum_bitcast_fusion), calls=%async_computation.1 | async-start | bytes 1048576 | tf_op jit(solution)/shard_map/all_to_all | solution.py:47
  32.0 0.3 fusion.54
  32.3 17.4 %all-to-all-done.1 = f32[8,4,4,4,130]{4,3,2,1,0:T(4,128)S(1)} async-done(((f32[8,4,4,4,130]{4,3,2,1,0:T(4,128)}), f32[8,4,4,4,130]{4,3,2,1,0:T(4,128)S(1)}, u32[]{:S(2)}, u32[]{:S(2)}) %all-to-all-start.1) | async-done | bytes 266272 | tf_op jit(solution)/shard_map/all_to_all | solution.py:47
  49.7 0.3 fusion.52
  49.9 0.5 copy.84
  50.4 0.5 copy.67
  51.0 0.2 fusion.29
  51.2 0.2 copy.63
  51.4 0.2 fusion.21
  51.7 0.2 fusion.7
  51.9 1.3 broadcast_in_dim.122
  53.2 11.3 %all-to-all-start.2 = ((bf16[64,4,2176]{2,1,0:T(4,128)(2,1)}), bf16[64,4,2176]{2,1,0:T(4,128)(2,1)}, u32[]{:S(2)}, u32[]{:S(2)}) async-start(bf16[64,4,2176]{2,1,0:T(4,128)(2,1)} %broadcast_in_dim.122), calls=%async_computation.2 | async-start | bytes 2228224 | tf_op jit(solution)/shard_map/all_to_all | solution.py:76
  64.6 0.5 broadcast.138
  65.1 0.7 reduce.8
  66.0 0.3 reduce-window.9
  67.0 1.4 scatter_custom_fusion
  68.4 0.7 gather_fusion
  69.2 24.1 %all-to-all-done.2 = bf16[64,4,2176]{2,1,0:T(4,128)(2,1)} async-done(((bf16[64,4,2176]{2,1,0:T(4,128)(2,1)}), bf16[64,4,2176]{2,1,0:T(4,128)(2,1)}, u32[]{:S(2)}, u32[]{:S(2)}) %all-to-all-start.2) | async-done | bytes 1114144 | tf_op jit(solution)/shard_map/all_to_all | solution.py:76
  93.3 1.4 reshape.162
  94.7 1.8 %gather_fusion.1 = bf16[128,2176]{1,0:T(8,128)(2,1)} fusion(bf16[256,2176]{1,0:T(8,128)(2,1)S(1)} %reshape.162, s32[1024]{0:T(1024)S(1)} %pad_clamp_fusion), kind=kCustom, calls=%fused_computation.1 | custom fusion | bytes 1114624 | tf_op jit(solution)/shard_map/jit(_take)/gather | solution.py:109
  96.5 1.5 fusion.8
  98.0 1.3 broadcast_in_dim.124
  99.2 5.9 %all-to-all-start.3 = ((bf16[64,128,64]{1,2,0:T(8,128)(2,1)}), bf16[64,128,64]{1,2,0:T(8,128)(2,1)S(1)}, u32[]{:S(2)}, u32[]{:S(2)}) async-start(bf16[64,128,64]{1,2,0:T(8,128)(2,1)} %broadcast_in_dim.124), calls=%async_computation.3 | async-start | bytes 2097152 | tf_op jit(solution)/shard_map/all_to_all | solution.py:76
  105.2 2.3 %copy.69 = bf16[128,4096]{0,1:T(8,128)(2,1)} copy(bf16[128,4096]{1,0:T(8,128)(2,1)} %param.19) | data formatting | bytes 2097152 | tf_op args[9]
  107.4 0.9 slice_convert_fusion
  108.4 24.3 %all-to-all-done.3 = bf16[64,128,64]{1,2,0:T(8,128)(2,1)S(1)} async-done(((bf16[64,128,64]{1,2,0:T(8,128)(2,1)}), bf16[64,128,64]{1,2,0:T(8,128)(2,1)S(1)}, u32[]{:S(2)}, u32[]{:S(2)}) %all-to-all-start.3) | async-done | bytes 1048608 | tf_op jit(solution)/shard_map/all_to_all | solution.py:76
  132.7 0.6 multiply_reduce_fusion
  133.3 0.7 fusion.1
  134.0 0.5 convolution_bitcast_fusion
  134.5 0.7 copy-done.1
  135.2 0.5 fusion.2
  135.7 32.9 %all_to_all.25 = bf16[64,128,64]{1,2,0:T(8,128)(2,1)S(1)} all-to-all(bf16[64,128,64]{1,2,0:T(8,128)(2,1)S(1)} %fusion.2), channel_id=1, replica_groups=mesh['grp'=8,'req'=64] {'req'}, dimensions={0} | all-to-all | bytes 2097152 | tf_op jit(solution)/shard_map/all_to_all | solution.py:136
  168.6 0.2 convert_reduce_fusion
  168.9 0.9 scatter_custom_fusion.1
  169.8 0.7 copy.71
  (46 shorter events, 1.9 us)
Async XLA Ops:
  0.0 134.0 %copy-start = (bf16[2,4096,128]{2,1,0:T(8,128)(2,1)S(1)}, bf16[2,4096,128]{2,1,0:T(8,128)(2,1)}, u32[]{:S(2)}) copy-start(bf16[2,4096,128]{2,1,0:T(8,128)(2,1)} %param.18) | copy-start | bytes 6291460
  1.6 20.2 %all-to-all-start = ((bf16[8,4,2048]{2,1,0:T(4,128)(2,1)}), bf16[8,4,2048]{2,1,0:T(4,128)(2,1)S(1)}, u32[]{:S(2)}, u32[]{:S(2)}) async-start(bf16[8,4,2048]{2,1,0:T(4,128)(2,1)} %broadcast_in_dim.116), calls=%async_computation | async-start | bytes 262144 | tf_op jit(solution)/shard_map/all_to_all | solution.py:24
  23.3 8.6 %copy-start.6 = (bf16[64]{0:T(256)(128)(2,1)S(1)}, bf16[64]{0:T(256)(128)(2,1)}, u32[]{:S(2)}) copy-start(bf16[64]{0:T(256)(128)(2,1)} %param.17) | copy-start | bytes 388
  24.6 7.4 %copy-start.3 = (bf16[1,1,4,2048]{3,2,1,0:T(4,128)(2,1)S(1)}, bf16[1,1,4,2048]{3,2,1,0:T(4,128)(2,1)}, u32[]{:S(2)}) copy-start(bf16[1,1,4,2048]{3,2,1,0:T(4,128)(2,1)} %param.10) | copy-start | bytes 49156
  24.6 7.3 %copy-start.5 = (bf16[1,1,2,4,512]{4,3,2,1,0:T(4,128)(2,1)S(1)}, bf16[1,1,2,4,512]{4,3,2,1,0:T(4,128)(2,1)}, u32[]{:S(2)}) copy-start(bf16[1,1,2,4,512]{4,3,2,1,0:T(4,128)(2,1)} %param.11) | copy-start | bytes 24580
  28.4 21.3 %all-to-all-start.1 = ((f32[8,4,4,4,130]{4,3,2,1,0:T(4,128)}), f32[8,4,4,4,130]{4,3,2,1,0:T(4,128)S(1)}, u32[]{:S(2)}, u32[]{:S(2)}) async-start(f32[8,4,4,4,130]{4,3,2,1,0:T(4,128)} %maximum_bitcast_fusion), calls=%async_computation.1 | async-start | bytes 1048576 | tf_op jit(solution)/shard_map/all_to_all | solution.py:47
  51.4 13.7 %copy-start.4 = (s32[1,64]{1,0:T(1,128)S(1)}, s32[1,64]{1,0:T(1,128)}, u32[]{:S(2)}) copy-start(s32[1,64]{1,0:T(1,128)} %param.14) | copy-start | bytes 772
  51.4 15.2 %copy-start.2 = (bf16[1,256,64]{1,2,0:T(8,128)(2,1)S(1)}, bf16[1,256,64]{1,2,0:T(8,128)(2,1)}, u32[]{:S(2)}) copy-start(bf16[1,256,64]{1,2,0:T(8,128)(2,1)} %param.15) | copy-start | bytes 98308
  53.2 40.1 %all-to-all-start.2 = ((bf16[64,4,2176]{2,1,0:T(4,128)(2,1)}), bf16[64,4,2176]{2,1,0:T(4,128)(2,1)}, u32[]{:S(2)}, u32[]{:S(2)}) async-start(bf16[64,4,2176]{2,1,0:T(4,128)(2,1)} %broadcast_in_dim.122), calls=%async_computation.2 | async-start | bytes 2228224 | tf_op jit(solution)/shard_map/all_to_all | solution.py:76
  99.2 33.5 %all-to-all-start.3 = ((bf16[64,128,64]{1,2,0:T(8,128)(2,1)}), bf16[64,128,64]{1,2,0:T(8,128)(2,1)S(1)}, u32[]{:S(2)}, u32[]{:S(2)}) async-start(bf16[64,128,64]{1,2,0:T(8,128)(2,1)} %broadcast_in_dim.124), calls=%async_computation.3 | async-start | bytes 2097152 | tf_op jit(solution)/shard_map/all_to_all | solution.py:76
  134.0 1.2 copy-start.1

commit v8 on v7

--- a/solution.py
+++ b/solution.py
@@ -41,13 +41,17 @@
         value_rows,
         preferred_element_type=jnp.float32,
     )
-    packed = jnp.concatenate([weighted, local_max[..., None], local_sum[..., None]], axis=-1)
-    packed = packed.reshape(KVH, QH // KVH, member_count, slot_count, HD + 2)
-    packed = jnp.transpose(packed, (2, 0, 1, 3, 4))
+    def by_member(part):
+        split = part.reshape(KVH, QH // KVH, member_count, slot_count, -1)
+        return jnp.transpose(split, (2, 0, 1, 3, 4)).reshape(member_count, QH * slot_count, -1)
+
+    stats = jnp.concatenate([by_member(local_max[..., None]), by_member(local_sum[..., None])], axis=1)
+    packed = jnp.concatenate([by_member(weighted), jnp.transpose(stats, (0, 2, 1))], axis=1)
     parts = lax.all_to_all(packed, "grp", 0, 0, tiled=False)
-    part_acc = parts[..., :HD]
-    part_max = parts[..., HD]
-    part_sum = parts[..., HD + 1]
+    head_shape = (member_count, KVH, QH // KVH, slot_count)
+    part_acc = parts[:, : QH * slot_count].reshape(head_shape + (HD,))
+    part_max = parts[:, QH * slot_count, : QH * slot_count].reshape(head_shape)
+    part_sum = parts[:, QH * slot_count, QH * slot_count :].reshape(head_shape)
     own_heads = heads_of(own_queries)
     suffix_keys = own_suffix[0].reshape(slot_count, KVH, HD)
     suffix_values = own_suffix[1].reshape(slot_count, KVH, HD)

time: 171 us -> 161 us (0.942)
  the two profiles are of different devices: /device:TPU:8 before, /device:TPU:128 now
where the time goes in v8:
time: 161 us; the launch traced here: 160 us
  waiting for transfers between devices  64.1 us (40%)
  blocking collectives  33.5 us (21%)
  starting transfers between devices  32.6 us (20%)
  local copies, waits for them, and re-layouts  19.6 us (12%)
  other arithmetic  5.01 us (3%)
  matrix products  4.65 us (3%)
    all_to_all x2, waiting for transfers between devices, gather_rows(): return lax.all_to_all(spread, 'req', 0, 0, tiled=False)  50.3 us
    all_to_all x1, blocking collectives, body(): lax.all_to_all(blocks.astype(jnp.bfloat16), 'req', 0, 0, tiled=False)  33.5 us
    all_to_all x2, starting transfers between devices, gather_rows(): return lax.all_to_all(spread, 'req', 0, 0, tiled=False)  16.6 us
    all_to_all x1, waiting for transfers between devices, attend(): parts = lax.all_to_all(packed, 'grp', 0, 0, tiled=False)  10.6 us
    all_to_all x1, starting transfers between devices, attend(): all_queries = lax.all_to_all(spread, 'grp', 0, 0, tiled=False)  9.05 us
    all_to_all x1, starting transfers between devices, attend(): parts = lax.all_to_all(packed, 'grp', 0, 0, tiled=False)  7 us
    unnamed x17, local copies, waits for them, and re-layouts  3.62 us
    all_to_all x1, waiting for transfers between devices, attend(): all_queries = lax.all_to_all(spread, 'grp', 0, 0, tiled=False)  3.23 us
  transfers between devices with their start and end apart: 4, of which 4 were waited for; matrix products, arithmetic and copies ran while one was open for 7% of the time, Pallas kernels for 0%

profile of v8, /device:TPU:128, one launch (start us, length us, event | category | flops | bytes accessed | tf_op | source)
XLA Modules:
  0.0 159.9 jit_solution(17811710129266760850)
XLA Ops:
  0.0 1.6 broadcast_in_dim.114
  1.6 9.0 %all-to-all-start = ((bf16[8,4,2048]{2,1,0:T(4,128)(2,1)}), bf16[8,4,2048]{2,1,0:T(4,128)(2,1)S(1)}, u32[]{:S(2)}, u32[]{:S(2)}) async-start(bf16[8,4,2048]{2,1,0:T(4,128)(2,1)} %broadcast_in_dim.114), calls=%async_computation | async-start | bytes 262144 | tf_op jit(solution)/shard_map/all_to_all | solution.py:24
  10.6 1.2 fusion.49
  11.8 0.8 compare_reduce_fusion
  12.7 0.8 reshape_squeeze.20
  13.6 3.2 %all-to-all-done = bf16[8,4,2048]{2,1,0:T(4,128)(2,1)S(1)} async-done(((bf16[8,4,2048]{2,1,0:T(4,128)(2,1)}), bf16[8,4,2048]{2,1,0:T(4,128)(2,1)S(1)}, u32[]{:S(2)}, u32[]{:S(2)}) %all-to-all-start) | async-done | bytes 131104 | tf_op jit(solution)/shard_map/all_to_all | solution.py:24
  16.9 0.4 fusion.50
  17.4 0.3 fusion.10
  17.9 0.2 copy.58
  18.1 0.2 copy.57
  18.3 1.3 fusion.13
  19.8 0.8 copy.61
  20.6 7.0 %all-to-all-start.1 = ((f32[8,65,128]{2,1,0:T(8,128)}), f32[8,65,128]{2,1,0:T(8,128)S(1)}, u32[]{:S(2)}, u32[]{:S(2)}) async-start(f32[8,65,128]{2,1,0:T(8,128)} %copy.61), calls=%async_computation.1 | async-start | bytes 589824 | tf_op jit(solution)/shard_map/all_to_all | solution.py:50
  27.6 0.3 fusion.51
  28.0 10.6 %all-to-all-done.1 = f32[8,65,128]{2,1,0:T(8,128)S(1)} async-done(((f32[8,65,128]{2,1,0:T(8,128)}), f32[8,65,128]{2,1,0:T(8,128)S(1)}, u32[]{:S(2)}, u32[]{:S(2)}) %all-to-all-start.1) | async-done | bytes 266272 | tf_op jit(solution)/shard_map/all_to_all | solution.py:50
  39.1 0.1 fusion.21
  39.2 0.2 fusion.7
  39.4 1.3 broadcast_in_dim.120
  40.8 10.8 %all-to-all-start.2 = ((bf16[64,4,2176]{2,1,0:T(4,128)(2,1)}), bf16[64,4,2176]{2,1,0:T(4,128)(2,1)}, u32[]{:S(2)}, u32[]{:S(2)}) async-start(bf16[64,4,2176]{2,1,0:T(4,128)(2,1)} %broadcast_in_dim.120), calls=%async_computation.2 | async-start | bytes 2228224 | tf_op jit(solution)/shard_map/all_to_all | solution.py:80
  51.6 0.5 broadcast.143
  52.1 0.7 reduce.10
  52.9 0.1 broadcast_in_dim.105
  53.1 0.3 reduce-window.9
  53.6 0.1 reshape.190
  53.7 0.1 copy.51
  53.8 0.1 slice_reduce_fusion
  54.0 1.4 scatter_custom_fusion
  55.4 0.7 gather_fusion
  56.3 25.2 %all-to-all-done.2 = bf16[64,4,2176]{2,1,0:T(4,128)(2,1)} async-done(((bf16[64,4,2176]{2,1,0:T(4,128)(2,1)}), bf16[64,4,2176]{2,1,0:T(4,128)(2,1)}, u32[]{:S(2)}, u32[]{:S(2)}) %all-to-all-start.2) | async-done | bytes 1114144 | tf_op jit(solution)/shard_map/all_to_all | solution.py:80
  81.4 1.4 reshape.198
  82.8 1.8 %gather_fusion.1 = bf16[128,2176]{1,0:T(8,128)(2,1)} fusion(bf16[256,2176]{1,0:T(8,128)(2,1)S(1)} %reshape.198, s32[1024]{0:T(1024)S(1)} %pad_clamp_fusion), kind=kCustom, calls=%fused_computation.1 | custom fusion | bytes 1114624 | tf_op jit(solution)/shard_map/jit(_take)/gather | solution.py:113
  84.6 1.5 fusion.8
  86.1 1.3 broadcast_in_dim.122
  87.3 5.8 %all-to-all-start.3 = ((bf16[64,128,64]{1,2,0:T(8,128)(2,1)}), bf16[64,128,64]{1,2,0:T(8,128)(2,1)S(1)}, u32[]{:S(2)}, u32[]{:S(2)}) async-start(bf16[64,128,64]{1,2,0:T(8,128)(2,1)} %broadcast_in_dim.122), calls=%async_computation.3 | async-start | bytes 2097152 | tf_op jit(solution)/shard_map/all_to_all | solution.py:80
  93.1 2.3 %copy.65 = bf16[128,4096]{0,1:T(8,128)(2,1)} copy(bf16[128,4096]{1,0:T(8,128)(2,1)} %param.19) | data formatting | bytes 2097152 | tf_op args[9]
  95.4 0.9 slice_convert_fusion
  96.2 0.1 reshape.200
  96.4 25.1 %all-to-all-done.3 = bf16[64,128,64]{1,2,0:T(8,128)(2,1)S(1)} async-done(((bf16[64,128,64]{1,2,0:T(8,128)(2,1)}), bf16[64,128,64]{1,2,0:T(8,128)(2,1)S(1)}, u32[]{:S(2)}, u32[]{:S(2)}) %all-to-all-start.3) | async-done | bytes 1048608 | tf_op jit(solution)/shard_map/all_to_all | solution.py:80
  121.5 0.6 multiply_reduce_fusion
  122.0 0.7 fusion.1
  122.8 0.5 convolution_bitcast_fusion
  123.3 0.7 copy-done.1
  124.0 0.4 fusion.2
  124.4 33.5 %all_to_all.25 = bf16[64,128,64]{1,2,0:T(8,128)(2,1)S(1)} all-to-all(bf16[64,128,64]{1,2,0:T(8,128)(2,1)S(1)} %fusion.2), channel_id=1, replica_groups=mesh['grp'=8,'req'=64] {'req'}, dimensions={0} | all-to-all | bytes 2097152 | tf_op jit(solution)/shard_map/all_to_all | solution.py:140
  157.9 0.2 convert_reduce_fusion
  158.1 0.1 copy.66
  158.2 0.9 scatter_custom_fusion.1
  159.2 0.7 copy.67
  (52 shorter events, 1.8 us)
Async XLA Ops:
  0.0 122.7 %copy-start = (bf16[2,4096,128]{2,1,0:T(8,128)(2,1)S(1)}, bf16[2,4096,128]{2,1,0:T(8,128)(2,1)}, u32[]{:S(2)}) copy-start(bf16[2,4096,128]{2,1,0:T(8,128)(2,1)} %param.18) | copy-start | bytes 6291460
  1.6 15.3 %all-to-all-start = ((bf16[8,4,2048]{2,1,0:T(4,128)(2,1)}), bf16[8,4,2048]{2,1,0:T(4,128)(2,1)S(1)}, u32[]{:S(2)}, u32[]{:S(2)}) async-start(bf16[8,4,2048]{2,1,0:T(4,128)(2,1)} %broadcast_in_dim.114), calls=%async_computation | async-start | bytes 262144 | tf_op jit(solution)/shard_map/all_to_all | solution.py:24
  17.7 9.8 %copy-start.3 = (bf16[1,1,4,2048]{3,2,1,0:T(4,128)(2,1)S(1)}, bf16[1,1,4,2048]{3,2,1,0:T(4,128)(2,1)}, u32[]{:S(2)}) copy-start(bf16[1,1,4,2048]{3,2,1,0:T(4,128)(2,1)} %param.10) | copy-start | bytes 49156
  17.7 9.8 %copy-start.5 = (bf16[1,1,2,4,512]{4,3,2,1,0:T(4,128)(2,1)S(1)}, bf16[1,1,2,4,512]{4,3,2,1,0:T(4,128)(2,1)}, u32[]{:S(2)}) copy-start(bf16[1,1,2,4,512]{4,3,2,1,0:T(4,128)(2,1)} %param.11) | copy-start | bytes 24580
  17.8 10.2 %copy-start.6 = (bf16[64]{0:T(256)(128)(2,1)S(1)}, bf16[64]{0:T(256)(128)(2,1)}, u32[]{:S(2)}) copy-start(bf16[64]{0:T(256)(128)(2,1)} %param.17) | copy-start | bytes 388
  20.6 18.1 %all-to-all-start.1 = ((f32[8,65,128]{2,1,0:T(8,128)}), f32[8,65,128]{2,1,0:T(8,128)S(1)}, u32[]{:S(2)}, u32[]{:S(2)}) async-start(f32[8,65,128]{2,1,0:T(8,128)} %copy.61), calls=%async_computation.1 | async-start | bytes 589824 | tf_op jit(solution)/shard_map/all_to_all | solution.py:50
  38.9 13.2 %copy-start.4 = (s32[1,64]{1,0:T(1,128)S(1)}, s32[1,64]{1,0:T(1,128)}, u32[]{:S(2)}) copy-start(s32[1,64]{1,0:T(1,128)} %param.14) | copy-start | bytes 772
  39.1 14.6 %copy-start.2 = (bf16[1,256,64]{1,2,0:T(8,128)(2,1)S(1)}, bf16[1,256,64]{1,2,0:T(8,128)(2,1)}, u32[]{:S(2)}) copy-start(bf16[1,256,64]{1,2,0:T(8,128)(2,1)} %param.15) | copy-start | bytes 98308
  40.8 40.6 %all-to-all-start.2 = ((bf16[64,4,2176]{2,1,0:T(4,128)(2,1)}), bf16[64,4,2176]{2,1,0:T(4,128)(2,1)}, u32[]{:S(2)}, u32[]{:S(2)}) async-start(bf16[64,4,2176]{2,1,0:T(4,128)(2,1)} %broadcast_in_dim.120), calls=%async_computation.2 | async-start | bytes 2228224 | tf_op jit(solution)/shard_map/all_to_all | solution.py:80
  87.3 34.2 %all-to-all-start.3 = ((bf16[64,128,64]{1,2,0:T(8,128)(2,1)}), bf16[64,128,64]{1,2,0:T(8,128)(2,1)S(1)}, u32[]{:S(2)}, u32[]{:S(2)}) async-start(bf16[64,128,64]{1,2,0:T(8,128)(2,1)} %broadcast_in_dim.122), calls=%async_computation.3 | async-start | bytes 2097152 | tf_op jit(solution)/shard_map/all_to_all | solution.py:80
  122.8 1.2 copy-start.1
